TPU v7x, 512 devices: a whole 4x8x8 slice. The times are simulated.
512 devices in a mesh: seq: 64 (over z, y), head: 8 (over x, core).
Axes of the slice: x: 4, y: 8, z: 8, core: 2. Of those that a mesh axis runs over, the one named last changes fastest.
Arguments:
- queries: bfloat16 [2, 4096, 8192], P(None, 'seq', 'head'), may hold values from -10 to 10
- key_states: bfloat16 [2, 4096, 1024], P(None, ('seq', 'head')), may hold values from -10 to 10
- value_state_rows: bfloat16 [2, 4096, 1024], P(None, ('seq', 'head')), may hold values from -6 to 6
- grad_out: bfloat16 [2, 4096, 8192], P(None, 'seq', 'head'), may hold values from -6 to 6
- layouts: int32 [4, 128, 8], replicated, may hold values from 0 to 127, as said below
- plant_ids: int32 [128], replicated, may hold values from 0 to 3
Outputs:
- attended: bfloat16 [2, 4096, 8192], P(None, 'seq', 'head')
- query_grad: bfloat16 [2, 4096, 8192], P(None, 'seq', 'head')
- key_grad: bfloat16 [2, 4096, 1024], P(None, ('seq', 'head'))
- value_grad: bfloat16 [2, 4096, 1024], P(None, ('seq', 'head'))
Inputs may be any that keep to these rules, and one draw needn't show every extreme that they name: Entry 0 of layouts[p, q] is q and every entry is at most q. With owner(b) = b for b < 64 and 127 - b otherwise: if an entry b of layouts[p, q] has owner(b) = o other than owner(q) = d, then b = o when o < d and b = 127 - o when o > d.
All inputs are finite; a program needn't handle non-finite values.
Results may differ from a plain program's by a relative error of at most 0.011.
Values may be sent and summed in bfloat16 or wider, within the bound.
No kernel may reach another device: no remote copies, remote signals or barrier semaphores. Data moves between devices by JAX's collectives and lax.ppermute only.
A program may use at most 64 MiB of HBM per device.

v0:
```python
import jax
import jax.numpy as jnp
from jax import lax
from jax.sharding import PartitionSpec as P

HEAD_SIZE = 128
BLOCK_TOKENS_N = 64
KEY_LIST_SIZE = 8


def live_entries(listed_blocks):
    same_block = listed_blocks[:, None] == listed_blocks[None, :]
    ordinal = jnp.arange(listed_blocks.shape[0], dtype=jnp.int32)
    earlier = ordinal[None, :] < ordinal[:, None]
    return jnp.logical_not(jnp.any(same_block & earlier, axis=1))


def allowed_mask(listed_blocks, live_entry, qblock):
    offsets = jnp.arange(BLOCK_TOKENS_N, dtype=jnp.int32)
    causal = offsets[None, :] <= offsets[:, None]
    diagonal = listed_blocks == qblock
    allowed = live_entry[:, None, None] & (jnp.logical_not(diagonal)[:, None, None] | causal[None])
    return jnp.transpose(allowed, (1, 0, 2)).reshape(BLOCK_TOKENS_N, KEY_LIST_SIZE * BLOCK_TOKENS_N)


def attend_block(query_row_values, gradient_rows, keys_sel, values_sel, allowed, scaling):
    kv_heads = keys_sel.shape[2] // HEAD_SIZE
    head_groups = query_row_values.shape[1] // (kv_heads * HEAD_SIZE)
    query_head_rows = query_row_values.reshape(BLOCK_TOKENS_N, kv_heads, head_groups, HEAD_SIZE)
    gradient_heads = gradient_rows.reshape(BLOCK_TOKENS_N, kv_heads, head_groups, HEAD_SIZE)
    key_head_rows = keys_sel.reshape(KEY_LIST_SIZE * BLOCK_TOKENS_N, kv_heads, HEAD_SIZE)
    value_head_rows = values_sel.reshape(KEY_LIST_SIZE * BLOCK_TOKENS_N, kv_heads, HEAD_SIZE)
    scores = (
        jnp.einsum(
            "qhgd,khd->hgqk", query_head_rows, key_head_rows, preferred_element_type=jnp.float32
        )
        * scaling
    )
    scores = jnp.where(allowed[None, None], scores, -1e30)
    row_max = jnp.max(scores, axis=-1, keepdims=True)
    exponent = jnp.exp(scores - row_max)
    normed = exponent / jnp.sum(exponent, axis=-1, keepdims=True)
    weights = normed.astype(jnp.bfloat16)
    block_out = jnp.einsum(
        "hgqk,khd->qhgd", weights, value_head_rows, preferred_element_type=jnp.float32
    )
    block_out = block_out.astype(jnp.bfloat16).reshape(BLOCK_TOKENS_N, -1)
    grad_probs = jnp.einsum(
        "qhgd,khd->hgqk", gradient_heads, value_head_rows, preferred_element_type=jnp.float32
    )
    row_delta = jnp.sum(normed * grad_probs, axis=-1, keepdims=True)
    grad_scores = (normed * (grad_probs - row_delta)).astype(jnp.bfloat16)
    block_dq = (
        jnp.einsum("hgqk,khd->qhgd", grad_scores, key_head_rows, preferred_element_type=jnp.float32)
        * scaling
    )
    block_dq = block_dq.astype(jnp.bfloat16).reshape(BLOCK_TOKENS_N, -1)
    key_portion = (
        jnp.einsum(
            "hgqk,qhgd->khd", grad_scores, query_head_rows, preferred_element_type=jnp.float32
        )
        * scaling
    )
    value_portion = jnp.einsum(
        "hgqk,qhgd->khd", weights, gradient_heads, preferred_element_type=jnp.float32
    )
    key_portion = key_portion.reshape(KEY_LIST_SIZE, BLOCK_TOKENS_N, kv_heads * HEAD_SIZE)
    value_portion = value_portion.reshape(KEY_LIST_SIZE, BLOCK_TOKENS_N, kv_heads * HEAD_SIZE)
    return (block_out, block_dq, key_portion, value_portion)


def body(queries, key_states, value_state_rows, grad_out, layouts, plant_ids):
    scaling = HEAD_SIZE ** (-0.5)
    seq_count = lax.axis_size("seq")
    device = lax.axis_index("seq")
    count_of_blocks = layouts.shape[1]
    halfway = count_of_blocks // 2
    mine_keys, mine_values = (
        lax.all_to_all(key_states, "head", split_axis=2, concat_axis=1, tiled=True),
        lax.all_to_all(value_state_rows, "head", split_axis=2, concat_axis=1, tiled=True),
    )
    qblocks = jnp.stack([device, count_of_blocks - 1 - device])
    pick_block = jnp.arange(count_of_blocks, dtype=jnp.int32)[None, :] == qblocks[:, None]
    plant_of = jnp.sum(jnp.where(pick_block, plant_ids[None, :], 0), axis=1)
    pick_plant = jnp.arange(layouts.shape[0], dtype=jnp.int32)[None, :] == plant_of[:, None]
    picked = pick_plant[:, :, None, None] & pick_block[:, None, :, None]
    listed_all = jnp.sum(jnp.where(picked, layouts[None], 0), axis=(1, 2))
    owners = jnp.where(listed_all < halfway, listed_all, count_of_blocks - 1 - listed_all)
    upper_half = (listed_all >= halfway).astype(jnp.int32)
    slot_of = jnp.where(owners == device, seq_count + upper_half, owners)
    pool_keys, pool_values = (
        lax.all_gather(mine_keys, "seq", axis=0, tiled=True),
        lax.all_gather(mine_values, "seq", axis=0, tiled=True),
    )
    pool_index = 2 * owners + upper_half
    width = mine_keys.shape[2]
    key_buffer = jnp.zeros((seq_count + 2, BLOCK_TOKENS_N, width), jnp.float32)
    value_buffer = jnp.zeros((seq_count + 2, BLOCK_TOKENS_N, width), jnp.float32)
    slot_ids = jnp.arange(seq_count + 2, dtype=jnp.int32)
    outputs = []
    query_grads = []
    for which_half in range(2):
        listed_blocks = listed_all[which_half]
        live_entry = live_entries(listed_blocks)
        allowed = allowed_mask(listed_blocks, live_entry, qblocks[which_half])
        chosen_index = pool_index[which_half]
        block_out, block_dq, key_portion, value_portion = attend_block(
            queries[which_half],
            grad_out[which_half],
            pool_keys[chosen_index],
            pool_values[chosen_index],
            allowed,
            scaling,
        )
        outputs.append(block_out)
        query_grads.append(block_dq)
        routing = (
            (slot_ids[:, None] == slot_of[which_half][None, :]) & live_entry[None, :]
        ).astype(jnp.float32)
        key_buffer = key_buffer + jnp.einsum(
            "sj,jbf->sbf", routing, key_portion, precision=lax.Precision.HIGHEST
        )
        value_buffer = value_buffer + jnp.einsum(
            "sj,jbf->sbf", routing, value_portion, precision=lax.Precision.HIGHEST
        )
    back_keys, back_values = (
        lax.all_to_all(
            key_buffer[:seq_count].astype(jnp.bfloat16),
            "seq",
            split_axis=0,
            concat_axis=0,
            tiled=True,
        ).astype(jnp.float32),
        lax.all_to_all(
            value_buffer[:seq_count].astype(jnp.bfloat16),
            "seq",
            split_axis=0,
            concat_axis=0,
            tiled=True,
        ).astype(jnp.float32),
    )
    from_higher = (jnp.arange(seq_count, dtype=jnp.int32) > device).astype(jnp.float32)[
        :, None, None
    ]
    from_lower = 1.0 - from_higher
    lower_key = key_buffer[seq_count] + jnp.sum(back_keys * from_higher, axis=0)
    upper_key = key_buffer[seq_count + 1] + jnp.sum(back_keys * from_lower, axis=0)
    lower_value = value_buffer[seq_count] + jnp.sum(back_values * from_higher, axis=0)
    upper_value = value_buffer[seq_count + 1] + jnp.sum(back_values * from_lower, axis=0)
    key_total = jnp.stack([lower_key, upper_key]).astype(jnp.bfloat16)
    value_total = jnp.stack([lower_value, upper_value]).astype(jnp.bfloat16)
    key_grad, value_grad = (
        lax.all_to_all(key_total, "head", split_axis=1, concat_axis=2, tiled=True),
        lax.all_to_all(value_total, "head", split_axis=1, concat_axis=2, tiled=True),
    )
    return (jnp.stack(outputs), jnp.stack(query_grads), key_grad, value_grad)


def solution(mesh):
    in_specs = (
        P(None, "seq", "head"),
        P(None, ("seq", "head"), None),
        P(None, ("seq", "head"), None),
        P(None, "seq", "head"),
        P(),
        P(),
    )
    out_specs = (
        P(None, "seq", "head"),
        P(None, "seq", "head"),
        P(None, ("seq", "head"), None),
        P(None, ("seq", "head"), None),
    )
    return jax.shard_map(body, mesh=mesh, in_specs=in_specs, out_specs=out_specs, check_vma=False)
```

profile of v0, /device:TPU:1, one launch (start us, length us, event | category | flops | bytes accessed | tf_op | source)
XLA Modules:
  0.0 306.1 jit_solution(1030200950925951874)
XLA Ops:
  7.3 1.1 copy.63
  8.9 13.9 %all_to_all.82 = bf16[8,2,1024]{2,1,0:T(2,128)(2,1)S(1)} all-to-all(bf16[8,2,1024]{2,1,0:T(2,128)(2,1)S(1)} %reshape.429), channel_id=1, replica_groups=mesh['seq'=64,'head'=8] {'head'}, dimensions={0} | all-to-all | bytes 65536 | tf_op jit(solution)/shard_map/all_to_all | solution.py:79
  25.4 7.8 %all_to_all.83 = bf16[8,2,1024]{2,1,0:T(2,128)(2,1)S(1)} all-to-all(bf16[8,2,1024]{2,1,0:T(2,128)(2,1)S(1)} %reshape.427), channel_id=1, replica_groups=mesh['seq'=64,'head'=8] {'head'}, dimensions={0} | all-to-all | bytes 65536 | tf_op jit(solution)/shard_map/all_to_all | solution.py:80
  36.9 66.1 %all-gather.5.cloned.1.call-done = bf16[128,64,128]{2,1,0:T(8,128)(2,1)} async-done(((bf16[2,64,128]{2,1,0:T(8,128)(2,1)}), bf16[128,64,128]{2,1,0:T(8,128)(2,1)}) %all-gather.5.cloned.1.call-update) | async-done | bytes 2097168 | tf_op jit(solution)/shard_map/all_gather | solution.py:92
  103.0 2.2 gather_fusion.3
  105.9 81.0 %all-gather.3.cloned.1.call-done = bf16[128,64,128]{2,1,0:T(8,128)(2,1)} async-done(((bf16[2,64,128]{2,1,0:T(8,128)(2,1)}), bf16[128,64,128]{2,1,0:T(8,128)(2,1)}) %all-gather.3.cloned.1.call-update) | async-done | bytes 2097168 | tf_op jit(solution)/shard_map/all_gather | solution.py:93
  186.9 2.2 gather_fusion.2
  190.8 1.0 fusion.8
  191.9 2.2 gather_fusion.1
  194.8 2.2 gather_fusion
  198.8 1.2 fusion.32
  200.0 1.3 convolution_add_fusion.1
  201.3 1.4 copy-done
  203.0 1.7 copy.77
  204.7 8.7 %all-to-all-start.2 = ((bf16[64,64,128]{2,1,0:T(8,128)(2,1)}), bf16[64,64,128]{2,1,0:T(8,128)(2,1)S(1)}, u32[]{:S(2)}, u32[]{:S(2)}) async-start(bf16[64,64,128]{2,1,0:T(8,128)(2,1)} %copy.77), calls=%async_computation.2 | async-start | bytes 2097152 | tf_op jit(solution)/shard_map/all_to_all | solution.py:127
  213.4 1.5 fusion.22
  215.6 1.2 fusion.29
  216.8 1.3 convolution_add_fusion
  218.1 1.4 copy-done.1
  219.8 1.6 copy.83
  221.5 15.4 %all-to-all-done.2 = bf16[64,64,128]{2,1,0:T(8,128)(2,1)S(1)} async-done(((bf16[64,64,128]{2,1,0:T(8,128)(2,1)}), bf16[64,64,128]{2,1,0:T(8,128)(2,1)S(1)}, u32[]{:S(2)}, u32[]{:S(2)}) %all-to-all-start.2) | async-done | bytes 1048608 | tf_op jit(solution)/shard_map/all_to_all | solution.py:127
  236.8 9.9 %all-to-all-start.4 = ((bf16[64,64,128]{2,1,0:T(8,128)(2,1)}), bf16[64,64,128]{2,1,0:T(8,128)(2,1)}, u32[]{:S(2)}, u32[]{:S(2)}) async-start(bf16[64,64,128]{2,1,0:T(8,128)(2,1)} %copy.83), calls=%async_computation.4 | async-start | bytes 2097152 | tf_op jit(solution)/shard_map/all_to_all | solution.py:134
  248.3 1.3 fusion.14
  249.8 1.3 fusion.12
  252.5 19.4 %all-to-all-done.4 = bf16[64,64,128]{2,1,0:T(8,128)(2,1)} async-done(((bf16[64,64,128]{2,1,0:T(8,128)(2,1)}), bf16[64,64,128]{2,1,0:T(8,128)(2,1)}, u32[]{:S(2)}, u32[]{:S(2)}) %all-to-all-start.4) | async-done | bytes 1048608 | tf_op jit(solution)/shard_map/all_to_all | solution.py:134
  271.9 2.0 fusion
  273.9 1.1 fusion.49
  275.8 9.5 %all-to-all-start.3 = ((bf16[2,64,128]{2,0,1:T(2,128)(2,1)}), bf16[2,64,128]{2,0,1:T(2,128)(2,1)S(1)}, u32[]{:S(2)}, u32[]{:S(2)}) async-start(bf16[2,64,128]{2,0,1:T(2,128)(2,1)} %pad_maximum_fusion.2), calls=%async_computation.3 | async-start | bytes 65536 | tf_op jit(solution)/shard_map/all_to_all | solution.py:153
  285.2 1.1 fusion.47
  287.0 2.9 all-to-all-done.3
  289.9 4.0 %all-to-all-start.5 = ((bf16[2,64,128]{2,0,1:T(2,128)(2,1)}), bf16[2,64,128]{2,0,1:T(2,128)(2,1)S(1)}, u32[]{:S(2)}, u32[]{:S(2)}) async-start(bf16[2,64,128]{2,0,1:T(2,128)(2,1)} %pad_maximum_fusion.3), calls=%async_computation.5 | async-start | bytes 65536 | tf_op jit(solution)/shard_map/all_to_all | solution.py:154
  295.2 3.4 %all-to-all-done.5 = bf16[2,64,128]{2,0,1:T(2,128)(2,1)S(1)} async-done(((bf16[2,64,128]{2,0,1:T(2,128)(2,1)}), bf16[2,64,128]{2,0,1:T(2,128)(2,1)S(1)}, u32[]{:S(2)}, u32[]{:S(2)}) %all-to-all-start.5) | async-done | bytes 32800 | tf_op jit(solution)/shard_map/all_to_all | solution.py:154
  (126 shorter events, 19.1 us)
Async XLA Ops:
  7.2 17.3 %copy-start.14 = (bf16[2,8,1024]{2,1,0:T(8,128)(2,1)S(1)}, bf16[2,8,1024]{2,1,0:T(8,128)(2,1)}, u32[]{:S(2)}) copy-start(bf16[2,8,1024]{2,1,0:T(8,128)(2,1)} %param.8) | copy-start | bytes 98308
  7.2 27.7 %copy-start.26 = (s32[128]{0:T(128)S(1)}, s32[128]{0:T(128)}, u32[]{:S(2)}) copy-start(s32[128]{0:T(128)} %param.11) | copy-start | bytes 1540
  7.2 28.1 %copy-start.15 = (s32[4,128,8]{1,2,0:T(8,128)S(1)}, s32[4,128,8]{1,2,0:T(8,128)}, u32[]{:S(2)}) copy-start(s32[4,128,8]{1,2,0:T(8,128)} %param.10) | copy-start | bytes 49156
  7.2 29.3 %copy-start.5 = (bf16[2,64,1024]{2,1,0:T(8,128)(2,1)S(1)}, bf16[2,64,1024]{2,1,0:T(8,128)(2,1)}, u32[]{:S(2)}) copy-start(bf16[2,64,1024]{2,1,0:T(8,128)(2,1)} %param.6) | copy-start | bytes 786436
  7.2 95.8 %all-gather.5.cloned.1.call-start = ((), (), s32[]{:S(2)}) async-start(), calls=%async_computation.7 | async-start | bytes 2129920 | tf_op jit(solution)/shard_map/all_gather | solution.py:92
  22.8 13.8 %copy-start.6 = (bf16[2,64,1024]{2,1,0:T(8,128)(2,1)S(1)}, bf16[2,64,1024]{2,1,0:T(8,128)(2,1)}, u32[]{:S(2)}) copy-start(bf16[2,64,1024]{2,1,0:T(8,128)(2,1)} %param.9) | copy-start | bytes 786436
  24.4 162.5 %all-gather.3.cloned.1.call-start = ((), (), s32[]{:S(2)}) async-start(), calls=%async_computation.6 | async-start | bytes 2129920 | tf_op jit(solution)/shard_map/all_gather | solution.py:93
  36.0 162.8 %copy-start.20 = (pred[8]{0:T(512)(128)(4,1)}, pred[8]{0:T(512)(128)(4,1)S(1)}, u32[]{:S(2)}) copy-start(pred[8]{0:T(512)(128)(4,1)S(1)} %not.36) | copy-start | bytes 28
  36.0 164.0 %copy-start.22 = (pred[8]{0:T(512)(128)(4,1)}, pred[8]{0:T(512)(128)(4,1)S(1)}, u32[]{:S(2)}) copy-start(pred[8]{0:T(512)(128)(4,1)S(1)} %not.38) | copy-start | bytes 28
  36.7 160.3 %copy-start.8 = (bf16[8,8,8,128]{3,2,1,0:T(8,128)(2,1)}, bf16[8,8,8,128]{3,2,1,0:T(8,128)(2,1)S(1)}, u32[]{:S(2)}) copy-start(bf16[8,8,8,128]{3,2,1,0:T(8,128)(2,1)S(1)} %copy.87) | copy-start | bytes 393220
  36.7 152.7 %copy-start.10 = (bf16[8,8,8,128]{3,2,1,0:T(8,128)(2,1)}, bf16[8,8,8,128]{3,2,1,0:T(8,128)(2,1)S(1)}, u32[]{:S(2)}) copy-start(bf16[8,8,8,128]{3,2,1,0:T(8,128)(2,1)S(1)} %copy.88) | copy-start | bytes 393220
  36.8 162.0 %copy-start.16 = (s32[8]{0:T(128)}, s32[8]{0:T(128)S(1)}, u32[]{:S(2)}) copy-start(s32[8]{0:T(128)S(1)} %get-tuple-element.21) | copy-start | bytes 100
  36.8 163.2 %copy-start.18 = (s32[8]{0:T(128)}, s32[8]{0:T(128)S(1)}, u32[]{:S(2)}) copy-start(s32[8]{0:T(128)S(1)} %get-tuple-element.20) | copy-start | bytes 100
  189.1 0.7 copy-start.11
  190.1 0.8 copy-start.2
  198.0 0.8 copy-start.3
  198.0 2.0 copy-start.7
  201.3 1.4 copy-start
  204.7 32.1 %all-to-all-start.2 = ((bf16[64,64,128]{2,1,0:T(8,128)(2,1)}), bf16[64,64,128]{2,1,0:T(8,128)(2,1)S(1)}, u32[]{:S(2)}, u32[]{:S(2)}) async-start(bf16[64,64,128]{2,1,0:T(8,128)(2,1)} %copy.77), calls=%async_computation.2 | async-start | bytes 2097152 | tf_op jit(solution)/shard_map/all_to_all | solution.py:127
  213.4 1.5 copy-start.9
  214.9 0.7 copy-start.17
  214.9 0.7 copy-start.21
  215.5 1.3 copy-start.19
  215.5 1.3 copy-start.23
  218.1 1.4 copy-start.1
  219.8 27.9 %copy-start.12 = (bf16[8,64,128]{2,1,0:T(8,128)(2,1)S(1)}, bf16[8,64,128]{2,1,0:T(8,128)(2,1)}, u32[]{:S(2)}) copy-start(bf16[8,64,128]{2,1,0:T(8,128)(2,1)} %copy-done.11) | copy-start | bytes 393220
  236.8 35.1 %all-to-all-start.4 = ((bf16[64,64,128]{2,1,0:T(8,128)(2,1)}), bf16[64,64,128]{2,1,0:T(8,128)(2,1)}, u32[]{:S(2)}, u32[]{:S(2)}) async-start(bf16[64,64,128]{2,1,0:T(8,128)(2,1)} %copy.83), calls=%async_computation.4 | async-start | bytes 2097152 | tf_op jit(solution)/shard_map/all_to_all | solution.py:134
  249.8 1.5 copy-start.4
  249.8 22.1 %copy-start.24 = (f32[64]{0:T(128)S(1)}, f32[64]{0:T(128)}, u32[]{:S(2)}) copy-start(f32[64]{0:T(128)} %broadcast_subtract_fusion) | copy-start | bytes 772
  249.8 22.1 %copy-start.25 = (f32[64]{0:T(128)S(1)}, f32[64]{0:T(128)}, u32[]{:S(2)}) copy-start(f32[64]{0:T(128)} %compare_convert_fusion) | copy-start | bytes 772
  275.8 14.2 %all-to-all-start.3 = ((bf16[2,64,128]{2,0,1:T(2,128)(2,1)}), bf16[2,64,128]{2,0,1:T(2,128)(2,1)S(1)}, u32[]{:S(2)}, u32[]{:S(2)}) async-start(bf16[2,64,128]{2,0,1:T(2,128)(2,1)} %pad_maximum_fusion.2), calls=%async_computation.3 | async-start | bytes 65536 | tf_op jit(solution)/shard_map/all_to_all | solution.py:153
  289.9 8.7 %all-to-all-start.5 = ((bf16[2,64,128]{2,0,1:T(2,128)(2,1)}), bf16[2,64,128]{2,0,1:T(2,128)(2,1)S(1)}, u32[]{:S(2)}, u32[]{:S(2)}) async-start(bf16[2,64,128]{2,0,1:T(2,128)(2,1)} %pad_maximum_fusion.3), calls=%async_computation.5 | async-start | bytes 65536 | tf_op jit(solution)/shard_map/all_to_all | solution.py:154
  (1 other events, 0.7 us)
Sparse Core Ops, SparseCore 0:
  24.5 78.4 all-gather.4
  106.6 80.2 all-gather.2
where the time goes:
time: 307 us; the launch traced here: 306 us
  waiting for transfers between devices  188 us (61%)
  starting transfers between devices  32.1 us (10%)
  local copies, waits for them, and re-layouts  25.6 us (8%)
  blocking collectives  21.7 us (7%)
  between operations  14.8 us (5%)
  matrix products  13.3 us (4%)
  other arithmetic  10.4 us (3%)
    all_gather x1, waiting for transfers between devices, body(): lax.all_gather(mine_values, 'seq', axis=0, tiled=True)  81 us
    all_gather x1, waiting for transfers between devices, body(): lax.all_gather(mine_keys, 'seq', axis=0, tiled=True)  66.1 us
    all_to_all x1, waiting for transfers between devices, body(): lax.all_to_all(value_buffer[:seq_count].astype(jnp.bfloat16), 'seq', spli...  19.4 us
    all_to_all x1, waiting for transfers between devices, body(): lax.all_to_all(key_buffer[:seq_count].astype(jnp.bfloat16), 'seq', split_...  15.4 us
    all_to_all x1, blocking collectives, body(): lax.all_to_all(key_states, 'head', split_axis=2, concat_axis=1, tiled=True)  13.9 us
    all_to_all x1, starting transfers between devices, body(): lax.all_to_all(value_buffer[:seq_count].astype(jnp.bfloat16), 'seq', spli...  9.89 us
    all_to_all x1, starting transfers between devices, body(): lax.all_to_all(key_total, 'head', split_axis=1, concat_axis=2, tiled=True)  9.46 us
    all_to_all x1, starting transfers between devices, body(): lax.all_to_all(key_buffer[:seq_count].astype(jnp.bfloat16), 'seq', split_...  8.74 us
  transfers between devices with their start and end apart: 6, of which 6 were waited for; matrix products, arithmetic and copies ran while one was open for 7% of the time, Pallas kernels for 0%

commit v1 on v0

--- a/solution.py
+++ b/solution.py
@@ -75,10 +75,8 @@
     device = lax.axis_index("seq")
     count_of_blocks = layouts.shape[1]
     halfway = count_of_blocks // 2
-    mine_keys, mine_values = (
-        lax.all_to_all(key_states, "head", split_axis=2, concat_axis=1, tiled=True),
-        lax.all_to_all(value_state_rows, "head", split_axis=2, concat_axis=1, tiled=True),
-    )
+    stacked = jnp.stack([key_states, value_state_rows])
+    mine = lax.all_to_all(stacked, "head", split_axis=3, concat_axis=2, tiled=True)
     qblocks = jnp.stack([device, count_of_blocks - 1 - device])
     pick_block = jnp.arange(count_of_blocks, dtype=jnp.int32)[None, :] == qblocks[:, None]
     plant_of = jnp.sum(jnp.where(pick_block, plant_ids[None, :], 0), axis=1)
@@ -88,12 +86,14 @@
     owners = jnp.where(listed_all < halfway, listed_all, count_of_blocks - 1 - listed_all)
     upper_half = (listed_all >= halfway).astype(jnp.int32)
     slot_of = jnp.where(owners == device, seq_count + upper_half, owners)
-    pool_keys, pool_values = (
-        lax.all_gather(mine_keys, "seq", axis=0, tiled=True),
-        lax.all_gather(mine_values, "seq", axis=0, tiled=True),
+    dest = jnp.arange(seq_count, dtype=jnp.int32)
+    send_lower = (dest >= device)[:, None, None, None]
+    send = jnp.where(send_lower, mine[:, 0][None], mine[:, 1][None])
+    received = lax.all_to_all(send, "seq", split_axis=0, concat_axis=0, tiled=True)
+    pool = jnp.concatenate(
+        [received, jnp.stack([mine[:, 0], mine[:, 1]])], axis=0
     )
-    pool_index = 2 * owners + upper_half
-    width = mine_keys.shape[2]
+    width = mine.shape[3]
     key_buffer = jnp.zeros((seq_count + 2, BLOCK_TOKENS_N, width), jnp.float32)
     value_buffer = jnp.zeros((seq_count + 2, BLOCK_TOKENS_N, width), jnp.float32)
     slot_ids = jnp.arange(seq_count + 2, dtype=jnp.int32)
@@ -103,12 +103,12 @@
         listed_blocks = listed_all[which_half]
         live_entry = live_entries(listed_blocks)
         allowed = allowed_mask(listed_blocks, live_entry, qblocks[which_half])
-        chosen_index = pool_index[which_half]
+        chosen = pool[slot_of[which_half]]
         block_out, block_dq, key_portion, value_portion = attend_block(
             queries[which_half],
             grad_out[which_half],
-            pool_keys[chosen_index],
-            pool_values[chosen_index],
+            chosen[:, 0],
+            chosen[:, 1],
             allowed,
             scaling,
         )
@@ -123,37 +123,19 @@
         value_buffer = value_buffer + jnp.einsum(
             "sj,jbf->sbf", routing, value_portion, precision=lax.Precision.HIGHEST
         )
-    back_keys, back_values = (
-        lax.all_to_all(
-            key_buffer[:seq_count].astype(jnp.bfloat16),
-            "seq",
-            split_axis=0,
-            concat_axis=0,
-            tiled=True,
-        ).astype(jnp.float32),
-        lax.all_to_all(
-            value_buffer[:seq_count].astype(jnp.bfloat16),
-            "seq",
-            split_axis=0,
-            concat_axis=0,
-            tiled=True,
-        ).astype(jnp.float32),
-    )
-    from_higher = (jnp.arange(seq_count, dtype=jnp.int32) > device).astype(jnp.float32)[
-        :, None, None
-    ]
-    from_lower = 1.0 - from_higher
-    lower_key = key_buffer[seq_count] + jnp.sum(back_keys * from_higher, axis=0)
-    upper_key = key_buffer[seq_count + 1] + jnp.sum(back_keys * from_lower, axis=0)
-    lower_value = value_buffer[seq_count] + jnp.sum(back_values * from_higher, axis=0)
-    upper_value = value_buffer[seq_count + 1] + jnp.sum(back_values * from_lower, axis=0)
-    key_total = jnp.stack([lower_key, upper_key]).astype(jnp.bfloat16)
-    value_total = jnp.stack([lower_value, upper_value]).astype(jnp.bfloat16)
-    key_grad, value_grad = (
-        lax.all_to_all(key_total, "head", split_axis=1, concat_axis=2, tiled=True),
-        lax.all_to_all(value_total, "head", split_axis=1, concat_axis=2, tiled=True),
-    )
-    return (jnp.stack(outputs), jnp.stack(query_grads), key_grad, value_grad)
+    partials = jnp.stack([key_buffer[:seq_count], value_buffer[:seq_count]], axis=1)
+    back = lax.all_to_all(
+        partials.astype(jnp.bfloat16), "seq", split_axis=0, concat_axis=0, tiled=True
+    ).astype(jnp.float32)
+    source = jnp.arange(seq_count, dtype=jnp.int32)
+    from_higher = (source > device).astype(jnp.float32)[:, None, None, None]
+    from_lower = (source < device).astype(jnp.float32)[:, None, None, None]
+    own = jnp.stack([key_buffer[seq_count:], value_buffer[seq_count:]])
+    lower_total = own[:, 0] + jnp.sum(back * from_higher, axis=0)
+    upper_total = own[:, 1] + jnp.sum(back * from_lower, axis=0)
+    totals = jnp.stack([lower_total, upper_total], axis=1).astype(jnp.bfloat16)
+    grads = lax.all_to_all(totals, "head", split_axis=2, concat_axis=3, tiled=True)
+    return (jnp.stack(outputs), jnp.stack(query_grads), grads[0], grads[1])
 
 
 def solution(mesh):

time: 307 us -> 183 us (0.60)
  waiting for transfers between devices: 188 us -> 96.4 us
  blocking collectives: 21.7 us -> 0 us
  between operations: 14.8 us -> 1.24 us
  starting transfers between devices: 32.1 us -> 41.6 us
  local copies, waits for them, and re-layouts: 25.6 us -> 20.4 us
    all_gather x2 -> x0, waiting for transfers between devices: 147 us -> none  [the longest x1 81 us: body(): lax.all_gather(mine_values, 'seq', axis=0, tiled=True)]
    all_to_all x4, waiting for transfers between devices: 41 us -> 96.4 us  [the longest x1 45.7 us: body(): lax.all_to_all(send, 'seq', split_axis=0, concat_axis=0, tiled=True)]
    all_to_all x2 -> x0, blocking collectives: 21.7 us -> none  [the longest x1 13.9 us: body(): lax.all_to_all(key_states, 'head', split_axis=2, concat_axis=1, tiled=True)]
    all_to_all x4, starting transfers between devices: 32.1 us -> 41.6 us  [the longest x1 12.3 us: body(): lax.all_to_all(send, 'seq', split_axis=0, concat_axis=0, tiled=True)]
    another operation x4 -> x11, local copies, waits for them, and re-layouts: 0.24 us -> 6.88 us  [the longest x3 3.3 us: body(): jnp.stack([key_buffer[:seq_count], value_buffer[:seq_count]], axis=1)]
    gather x4 -> x2, local copies, waits for them, and re-layouts: 8.64 us -> 4.41 us  [body(): chosen = pool[slot_of[which_half]]]
    unnamed x66 -> x44, local copies, waits for them, and re-layouts: 8.57 us -> 4.71 us
  transfers between devices with their start and end apart: 6 -> 4, of which waited for: 6 -> 4; matrix products, arithmetic and copies ran while one was open for 7% -> 5% of each run, Pallas kernels for 0% -> 0%
where the time goes in v1:
time: 183 us; the launch traced here: 182 us
  waiting for transfers between devices  96.4 us (53%)
  starting transfers between devices  41.6 us (23%)
  local copies, waits for them, and re-layouts  20.4 us (11%)
  other arithmetic  11.8 us (6%)
  matrix products  10.6 us (6%)
    all_to_all x1, waiting for transfers between devices, body(): lax.all_to_all(send, 'seq', split_axis=0, concat_axis=0, tiled=True)  45.7 us
    all_to_all x1, waiting for transfers between devices, body(): lax.all_to_all(partials.astype(jnp.bfloat16), 'seq', split_axis=0, concat...  41.7 us
    all_to_all x1, starting transfers between devices, body(): lax.all_to_all(send, 'seq', split_axis=0, concat_axis=0, tiled=True)  12.3 us
    all_to_all x1, starting transfers between devices, body(): lax.all_to_all(partials.astype(jnp.bfloat16), 'seq', split_axis=0, concat...  10.7 us
    all_to_all x1, starting transfers between devices, body(): lax.all_to_all(stacked, 'head', split_axis=3, concat_axis=2, tiled=True)  10.1 us
    all_to_all x1, starting transfers between devices, body(): lax.all_to_all(totals, 'head', split_axis=2, concat_axis=3, tiled=True)  8.52 us
    all_to_all x1, waiting for transfers between devices, body(): lax.all_to_all(stacked, 'head', split_axis=3, concat_axis=2, tiled=True)  4.86 us
    unnamed x44, local copies, waits for them, and re-layouts  4.71 us
  transfers between devices with their start and end apart: 4, of which 4 were waited for; matrix products, arithmetic and copies ran while one was open for 5% of the time, Pallas kernels for 0%

profile of v1, /device:TPU:1, one launch (start us, length us, event | category | flops | bytes accessed | tf_op | source)
XLA Modules:
  0.0 182.0 jit_solution(14197767792075189323)
XLA Ops:
  0.6 0.8 pad_maximum_fusion.5
  1.4 0.7 copy.84
  2.1 1.7 reshape.416
  3.8 10.1 %all-to-all-start = ((bf16[8,2,2048]{2,1,0:T(2,128)(2,1)}), bf16[8,2,2048]{2,1,0:T(2,128)(2,1)S(1)}, u32[]{:S(2)}, u32[]{:S(2)}) async-start(bf16[8,2,2048]{2,1,0:T(2,128)(2,1)} %reshape.416), calls=%async_computation | async-start | bytes 131072 | tf_op jit(solution)/shard_map/all_to_all | solution.py:79
  13.9 4.9 %all-to-all-done = bf16[8,2,2048]{2,1,0:T(2,128)(2,1)S(1)} async-done(((bf16[8,2,2048]{2,1,0:T(2,128)(2,1)}), bf16[8,2,2048]{2,1,0:T(2,128)(2,1)S(1)}, u32[]{:S(2)}, u32[]{:S(2)}) %all-to-all-start) | async-done | bytes 65568 | tf_op jit(solution)/shard_map/all_to_all | solution.py:79
  18.8 1.2 reshape.417
  20.0 1.3 copy.85
  21.4 1.5 broadcast_select_fusion
  22.9 12.3 %all-to-all-start.1 = ((bf16[64,2,64,128]{3,2,1,0:T(8,128)(2,1)}), bf16[64,2,64,128]{3,2,1,0:T(8,128)(2,1)S(1)}, u32[]{:S(2)}, u32[]{:S(2)}) async-start(bf16[64,2,64,128]{3,2,1,0:T(8,128)(2,1)} %broadcast_select_fusion), calls=%async_computation.1 | async-start | bytes 4194304 | tf_op jit(solution)/shard_map/all_to_all | solution.py:92
  38.0 0.7 or_and_fusion.1
  38.6 45.7 %all-to-all-done.1 = bf16[64,2,64,128]{3,2,1,0:T(8,128)(2,1)S(1)} async-done(((bf16[64,2,64,128]{3,2,1,0:T(8,128)(2,1)}), bf16[64,2,64,128]{3,2,1,0:T(8,128)(2,1)S(1)}, u32[]{:S(2)}, u32[]{:S(2)}) %all-to-all-start.1) | async-done | bytes 2097184 | tf_op jit(solution)/shard_map/all_to_all | solution.py:92
  84.3 1.6 pad_maximum_fusion
  85.9 2.2 %gather_fusion.1 = bf16[8,2,64,128]{3,2,1,0:T(8,128)(2,1)S(1)} fusion(bf16[66,2,64,128]{3,2,1,0:T(8,128)(2,1)} %pad_maximum_fusion, s32[1024]{0:T(1024)S(1)} %get-tuple-element.42), kind=kCustom, calls=%fused_computation.1 | custom fusion | bytes 524320 | tf_op jit(solution)/shard_map/gather | solution.py:106
  88.2 2.2 %gather_fusion = bf16[8,2,64,128]{3,2,1,0:T(8,128)(2,1)S(1)} fusion(bf16[66,2,64,128]{3,2,1,0:T(8,128)(2,1)} %pad_maximum_fusion, s32[1024]{0:T(1024)S(1)} %get-tuple-element.43), kind=kCustom, calls=%fused_computation | custom fusion | bytes 524320 | tf_op jit(solution)/shard_map/gather | solution.py:106
  95.4 1.2 fusion.32
  96.6 1.3 convolution_add_fusion.1
  98.2 1.2 fusion.29
  99.4 1.3 convolution_add_fusion
  100.7 1.4 copy-done.1
  102.6 2.8 %copy.102 = bf16[64,2,64,128]{3,2,1,0:T(8,128)(2,1)} copy(bf16[64,2,64,128]{3,0,2,1:T(8,128)(2,1)S(1)} %pad_maximum_fusion.1) | data formatting | bytes 4194304 | tf_op jit(solution)/shard_map/stack | solution.py:126
  105.3 10.7 %all-to-all-start.2 = ((bf16[64,2,64,128]{3,2,1,0:T(8,128)(2,1)}), bf16[64,2,64,128]{3,2,1,0:T(8,128)(2,1)}, u32[]{:S(2)}, u32[]{:S(2)}) async-start(bf16[64,2,64,128]{3,2,1,0:T(8,128)(2,1)} %copy.102), calls=%async_computation.2 | async-start | bytes 4194304 | tf_op jit(solution)/shard_map/all_to_all | solution.py:127
  116.6 1.3 fusion.11
  119.6 0.7 pad_maximum_fusion.2
  120.3 1.0 slice_bitcast_fusion.5
  121.3 1.0 slice_bitcast_fusion.4
  122.3 41.7 %all-to-all-done.2 = bf16[64,2,64,128]{3,2,1,0:T(8,128)(2,1)} async-done(((bf16[64,2,64,128]{3,2,1,0:T(8,128)(2,1)}), bf16[64,2,64,128]{3,2,1,0:T(8,128)(2,1)}, u32[]{:S(2)}, u32[]{:S(2)}) %all-to-all-start.2) | async-done | bytes 2097184 | tf_op jit(solution)/shard_map/all_to_all | solution.py:127
  163.9 2.4 %fusion = (f32[2,64,128]{2,1,0:T(8,128)S(1)}, f32[2,64,128]{2,1,0:T(8,128)S(1)}) fusion(bf16[64,2,64,128]{3,2,1,0:T(8,128)(2,1)} %all-to-all-done.2, f32[64]{0:T(128)S(1)} %copy-done.16, f32[64]{0:T(128)S(1)} %copy-done.15), kind=kLoop, calls=%fused_computation.4 | loop fusion | flops 5210112 | bytes 2228736 | tf_op jit(solution)/shard_map/reduce_sum | solution.py:134
  166.7 0.7 copy.103
  167.3 8.5 %all-to-all-start.3 = ((bf16[2,2,64,128]{3,1,0,2:T(2,128)(2,1)}), bf16[2,2,64,128]{3,1,0,2:T(2,128)(2,1)S(1)}, u32[]{:S(2)}, u32[]{:S(2)}) async-start(bf16[2,2,64,128]{3,1,0,2:T(2,128)(2,1)} %copy.103), calls=%async_computation.3 | async-start | bytes 131072 | tf_op jit(solution)/shard_map/all_to_all | solution.py:137
  175.9 0.7 pad_maximum_fusion.3
  176.6 4.1 %all-to-all-done.3 = bf16[2,2,64,128]{3,1,0,2:T(2,128)(2,1)S(1)} async-done(((bf16[2,2,64,128]{3,1,0,2:T(2,128)(2,1)}), bf16[2,2,64,128]{3,1,0,2:T(2,128)(2,1)S(1)}, u32[]{:S(2)}, u32[]{:S(2)}) %all-to-all-start.3) | async-done | bytes 65568 | tf_op jit(solution)/shard_map/all_to_all | solution.py:137
  180.8 0.6 copy.144
  (102 shorter events, 11.4 us)
Async XLA Ops:
  3.8 15.0 %all-to-all-start = ((bf16[8,2,2048]{2,1,0:T(2,128)(2,1)}), bf16[8,2,2048]{2,1,0:T(2,128)(2,1)S(1)}, u32[]{:S(2)}, u32[]{:S(2)}) async-start(bf16[8,2,2048]{2,1,0:T(2,128)(2,1)} %reshape.416), calls=%async_computation | async-start | bytes 131072 | tf_op jit(solution)/shard_map/all_to_all | solution.py:79
  22.9 12.4 %copy-start.17 = (s32[128]{0:T(128)S(1)}, s32[128]{0:T(128)}, u32[]{:S(2)}) copy-start(s32[128]{0:T(128)} %param.11) | copy-start | bytes 1540
  22.9 12.8 %copy-start.8 = (s32[4,128,8]{1,2,0:T(8,128)S(1)}, s32[4,128,8]{1,2,0:T(8,128)}, u32[]{:S(2)}) copy-start(s32[4,128,8]{1,2,0:T(8,128)} %param.10) | copy-start | bytes 49156
  22.9 14.2 %copy-start.2 = (bf16[2,64,1024]{2,1,0:T(8,128)(2,1)S(1)}, bf16[2,64,1024]{2,1,0:T(8,128)(2,1)}, u32[]{:S(2)}) copy-start(bf16[2,64,1024]{2,1,0:T(8,128)(2,1)} %param.6) | copy-start | bytes 786436
  22.9 14.3 %copy-start.3 = (bf16[2,64,1024]{2,1,0:T(8,128)(2,1)S(1)}, bf16[2,64,1024]{2,1,0:T(8,128)(2,1)}, u32[]{:S(2)}) copy-start(bf16[2,64,1024]{2,1,0:T(8,128)(2,1)} %param.9) | copy-start | bytes 786436
  22.9 61.4 %all-to-all-start.1 = ((bf16[64,2,64,128]{3,2,1,0:T(8,128)(2,1)}), bf16[64,2,64,128]{3,2,1,0:T(8,128)(2,1)S(1)}, u32[]{:S(2)}, u32[]{:S(2)}) async-start(bf16[64,2,64,128]{3,2,1,0:T(8,128)(2,1)} %broadcast_select_fusion), calls=%async_computation.1 | async-start | bytes 4194304 | tf_op jit(solution)/shard_map/all_to_all | solution.py:92
  36.3 0.5 copy-start.11
  36.3 0.5 copy-start.13
  90.4 3.8 %copy-start.4 = (bf16[8,1,64,128]{3,2,1,0:T(8,128)(2,1)}, bf16[8,1,64,128]{3,2,1,0:T(8,128)(2,1)S(1)}, u32[]{:S(2)}) copy-start(bf16[8,1,64,128]{3,2,1,0:T(8,128)(2,1)S(1)} %get-tuple-element.11) | copy-start | bytes 393220
  90.4 1.3 copy-start.6
  92.2 0.8 copy-start.7
  94.6 0.7 copy-start.9
  94.6 0.7 copy-start.12
  95.0 1.6 copy-start.10
  95.0 1.6 copy-start.14
  97.9 1.5 copy-start
  100.7 1.4 copy-start.1
  105.3 58.6 %all-to-all-start.2 = ((bf16[64,2,64,128]{3,2,1,0:T(8,128)(2,1)}), bf16[64,2,64,128]{3,2,1,0:T(8,128)(2,1)}, u32[]{:S(2)}, u32[]{:S(2)}) async-start(bf16[64,2,64,128]{3,2,1,0:T(8,128)(2,1)} %copy.102), calls=%async_computation.2 | async-start | bytes 4194304 | tf_op jit(solution)/shard_map/all_to_all | solution.py:127
  116.6 2.0 %copy-start.5 = (bf16[8,1,64,128]{3,2,1,0:T(8,128)(2,1)S(1)}, bf16[8,1,64,128]{3,2,1,0:T(8,128)(2,1)}, u32[]{:S(2)}) copy-start(bf16[8,1,64,128]{3,2,1,0:T(8,128)(2,1)} %copy-done.4) | copy-start | bytes 393220
  118.9 45.0 %copy-start.15 = (f32[64]{0:T(128)S(1)}, f32[64]{0:T(128)}, u32[]{:S(2)}) copy-start(f32[64]{0:T(128)} %get-tuple-element.40) | copy-start | bytes 772
  118.9 45.0 %copy-start.16 = (f32[64]{0:T(128)S(1)}, f32[64]{0:T(128)}, u32[]{:S(2)}) copy-start(f32[64]{0:T(128)} %get-tuple-element.41) | copy-start | bytes 772
  167.3 13.4 %all-to-all-start.3 = ((bf16[2,2,64,128]{3,1,0,2:T(2,128)(2,1)}), bf16[2,2,64,128]{3,1,0,2:T(2,128)(2,1)S(1)}, u32[]{:S(2)}, u32[]{:S(2)}) async-start(bf16[2,2,64,128]{3,1,0,2:T(2,128)(2,1)} %copy.103), calls=%async_computation.3 | async-start | bytes 131072 | tf_op jit(solution)/shard_map/all_to_all | solution.py:137

commit v2 on v1

v2 whole, which is shorter than its diff:
```python
import jax
import jax.numpy as jnp
from jax import lax
from jax.sharding import PartitionSpec as P
import functools
from jax.experimental import pallas as pl
from jax.experimental.pallas import tpu as pltpu

HEAD_SIZE = 128
BLOCK_TOKENS_N = 64
KEY_LIST_SIZE = 8


def live_entries(listed_blocks):
    same_block = listed_blocks[:, None] == listed_blocks[None, :]
    ordinal = jnp.arange(listed_blocks.shape[0], dtype=jnp.int32)
    earlier = ordinal[None, :] < ordinal[:, None]
    return jnp.logical_not(jnp.any(same_block & earlier, axis=1))


def allowed_mask(listed_blocks, live_entry, qblock):
    offsets = jnp.arange(BLOCK_TOKENS_N, dtype=jnp.int32)
    causal = offsets[None, :] <= offsets[:, None]
    diagonal = listed_blocks == qblock
    allowed = live_entry[:, None, None] & (jnp.logical_not(diagonal)[:, None, None] | causal[None])
    return jnp.transpose(allowed, (1, 0, 2)).reshape(BLOCK_TOKENS_N, KEY_LIST_SIZE * BLOCK_TOKENS_N)


def attention_kernel(meta_ref, q_ref, do_ref, recv_ref, mine_ref,
                     out_ref, dq_ref, send_ref, own_ref, acc_ref, *, scaling):
    seq_count = recv_ref.shape[0]
    groups = q_ref.shape[2] // HEAD_SIZE
    rows = groups * BLOCK_TOKENS_N
    cols = KEY_LIST_SIZE * BLOCK_TOKENS_N
    acc_ref[...] = jnp.zeros_like(acc_ref)
    col = lax.broadcasted_iota(jnp.int32, (1, cols), 1)
    col_block = col // BLOCK_TOKENS_N
    key_pos = col % BLOCK_TOKENS_N
    query_pos = lax.broadcasted_iota(jnp.int32, (rows, 1), 0) % BLOCK_TOKENS_N
    for half in range(2):
        keys, values = [], []
        live_row = jnp.zeros((1, cols), jnp.int32)
        diag_row = jnp.zeros((1, cols), jnp.int32)
        for j in range(KEY_LIST_SIZE):
            slot = meta_ref[half, 0, j]
            from_recv = slot < seq_count
            r = jnp.minimum(slot, seq_count - 1)
            m = jnp.maximum(slot - seq_count, 0)
            keys.append(jnp.where(from_recv, recv_ref[r, 0], mine_ref[0, m]))
            values.append(jnp.where(from_recv, recv_ref[r, 1], mine_ref[1, m]))
            live_row = jnp.where(col_block == j, meta_ref[half, 1, j], live_row)
            diag_row = jnp.where(col_block == j, meta_ref[half, 2, j], diag_row)
        key_all = jnp.concatenate(keys, axis=0)
        value_all = jnp.concatenate(values, axis=0)
        query_all = jnp.concatenate(
            [q_ref[half, :, g * HEAD_SIZE:(g + 1) * HEAD_SIZE] for g in range(groups)], axis=0)
        grad_all = jnp.concatenate(
            [do_ref[half, :, g * HEAD_SIZE:(g + 1) * HEAD_SIZE] for g in range(groups)], axis=0)
        allowed = (live_row != 0) & ((diag_row == 0) | (key_pos <= query_pos))
        nt = (((1,), (1,)), ((), ()))
        tn = (((0,), (0,)), ((), ()))
        scores = lax.dot_general(query_all, key_all, nt, preferred_element_type=jnp.float32) * scaling
        scores = jnp.where(allowed, scores, -1e30)
        row_max = jnp.max(scores, axis=1, keepdims=True)
        exponent = jnp.exp(scores - row_max)
        normed = exponent / jnp.sum(exponent, axis=1, keepdims=True)
        weights = normed.astype(jnp.bfloat16)
        block_out = jnp.dot(weights, value_all, preferred_element_type=jnp.float32).astype(out_ref.dtype)
        grad_probs = lax.dot_general(grad_all, value_all, nt, preferred_element_type=jnp.float32)
        row_delta = jnp.sum(normed * grad_probs, axis=1, keepdims=True)
        grad_scores = (normed * (grad_probs - row_delta)).astype(jnp.bfloat16)
        block_dq = (jnp.dot(grad_scores, key_all, preferred_element_type=jnp.float32) * scaling).astype(dq_ref.dtype)
        for g in range(groups):
            out_ref[half, :, g * HEAD_SIZE:(g + 1) * HEAD_SIZE] = block_out[g * BLOCK_TOKENS_N:(g + 1) * BLOCK_TOKENS_N]
            dq_ref[half, :, g * HEAD_SIZE:(g + 1) * HEAD_SIZE] = block_dq[g * BLOCK_TOKENS_N:(g + 1) * BLOCK_TOKENS_N]
        key_portion = lax.dot_general(grad_scores, query_all, tn, preferred_element_type=jnp.float32) * scaling
        value_portion = lax.dot_general(weights, grad_all, tn, preferred_element_type=jnp.float32)
        for j in range(KEY_LIST_SIZE):
            slot = meta_ref[half, 0, j]
            keep = meta_ref[half, 1, j] != 0
            piece = slice(j * BLOCK_TOKENS_N, (j + 1) * BLOCK_TOKENS_N)
            acc_ref[slot, 0] += jnp.where(keep, key_portion[piece], 0.0)
            acc_ref[slot, 1] += jnp.where(keep, value_portion[piece], 0.0)
    send_ref[...] = acc_ref[:seq_count].astype(send_ref.dtype)
    own_ref[...] = acc_ref[seq_count:]


def attention_call(meta, queries, grad_out, received, mine, scaling):
    seq_count = received.shape[0]
    width = received.shape[3]
    vmem = pltpu.VMEM
    smem = pltpu.SMEM
    return pl.pallas_call(
        functools.partial(attention_kernel, scaling=scaling),
        out_shape=(
            jax.ShapeDtypeStruct(queries.shape, queries.dtype),
            jax.ShapeDtypeStruct(queries.shape, queries.dtype),
            jax.ShapeDtypeStruct(received.shape, received.dtype),
            jax.ShapeDtypeStruct((2, 2, BLOCK_TOKENS_N, width), jnp.float32),
        ),
        in_specs=[pl.BlockSpec(memory_space=smem)] + [pl.BlockSpec(memory_space=vmem)] * 4,
        out_specs=[pl.BlockSpec(memory_space=vmem)] * 4,
        scratch_shapes=[pltpu.VMEM((seq_count + 2, 2, BLOCK_TOKENS_N, width), jnp.float32)],
        compiler_params=pltpu.CompilerParams(vmem_limit_bytes=48 * 1024 * 1024),
    )(meta, queries, grad_out, received, mine)


def body(queries, key_states, value_state_rows, grad_out, layouts, plant_ids):
    scaling = HEAD_SIZE ** (-0.5)
    seq_count = lax.axis_size("seq")
    device = lax.axis_index("seq")
    count_of_blocks = layouts.shape[1]
    halfway = count_of_blocks // 2
    stacked = jnp.stack([key_states, value_state_rows])
    mine = lax.all_to_all(stacked, "head", split_axis=3, concat_axis=2, tiled=True)
    qblocks = jnp.stack([device, count_of_blocks - 1 - device])
    pick_block = jnp.arange(count_of_blocks, dtype=jnp.int32)[None, :] == qblocks[:, None]
    plant_of = jnp.sum(jnp.where(pick_block, plant_ids[None, :], 0), axis=1)
    pick_plant = jnp.arange(layouts.shape[0], dtype=jnp.int32)[None, :] == plant_of[:, None]
    picked = pick_plant[:, :, None, None] & pick_block[:, None, :, None]
    listed_all = jnp.sum(jnp.where(picked, layouts[None], 0), axis=(1, 2))
    owners = jnp.where(listed_all < halfway, listed_all, count_of_blocks - 1 - listed_all)
    upper_half = (listed_all >= halfway).astype(jnp.int32)
    slot_of = jnp.where(owners == device, seq_count + upper_half, owners)
    live = jnp.stack([live_entries(listed_all[h]) for h in range(2)]).astype(jnp.int32)
    diagonal = (listed_all == qblocks[:, None]).astype(jnp.int32)
    meta = jnp.stack([slot_of, live, diagonal], axis=1)
    dest = jnp.arange(seq_count, dtype=jnp.int32)
    send_lower = (dest >= device)[:, None, None, None]
    send = jnp.where(send_lower, mine[:, 0][None], mine[:, 1][None])
    received = lax.all_to_all(send, "seq", split_axis=0, concat_axis=0, tiled=True)
    outputs, query_grads, partials, own = attention_call(
        meta, queries, grad_out, received, mine, scaling
    )
    back = lax.all_to_all(partials, "seq", split_axis=0, concat_axis=0, tiled=True).astype(
        jnp.float32
    )
    source = jnp.arange(seq_count, dtype=jnp.int32)
    from_higher = (source > device).astype(jnp.float32)[:, None, None, None]
    from_lower = (source < device).astype(jnp.float32)[:, None, None, None]
    lower_total = own[0] + jnp.sum(back * from_higher, axis=0)
    upper_total = own[1] + jnp.sum(back * from_lower, axis=0)
    totals = jnp.stack([lower_total, upper_total], axis=1).astype(jnp.bfloat16)
    grads = lax.all_to_all(totals, "head", split_axis=2, concat_axis=3, tiled=True)
    return (outputs, query_grads, grads[0], grads[1])


def solution(mesh):
    in_specs = (
        P(None, "seq", "head"),
        P(None, ("seq", "head"), None),
        P(None, ("seq", "head"), None),
        P(None, "seq", "head"),
        P(),
        P(),
    )
    out_specs = (
        P(None, "seq", "head"),
        P(None, "seq", "head"),
        P(None, ("seq", "head"), None),
        P(None, ("seq", "head"), None),
    )
    return jax.shard_map(body, mesh=mesh, in_specs=in_specs, out_specs=out_specs, check_vma=False)
```

time: 183 us -> 165 us (0.902)
  local copies, waits for them, and re-layouts: 20.4 us -> 7.77 us
  blocking collectives: 0 us -> 12.6 us
  matrix products: 10.6 us -> 0 us
  starting transfers between devices: 41.6 us -> 33.1 us
  other arithmetic: 11.8 us -> 4.04 us
  waiting for transfers between devices: 96.4 us -> 101 us
  Pallas kernels: 0 us -> 4.5 us
    all_to_all x0 -> x1, blocking collectives: none -> 12.6 us  [body(): lax.all_to_all(totals, 'head', split_axis=2, concat_axis=3, tiled=True)]
    dot_general x16 -> x0, matrix products: 10.6 us -> none  [the longest x2 2.47 us: body(): jnp.einsum('sj,jbf->sbf', routing, value_portion, precision=lax.Precision...]
    all_to_all x2 -> x1, starting transfers between devices: 19.2 us -> 10.9 us  [body(): lax.all_to_all(partials, 'seq', split_axis=0, concat_axis=0, tiled=True)]
    another operation x9 -> x0, local copies, waits for them, and re-layouts: 5.48 us -> none  [the longest x3 3.3 us: body(): jnp.stack([key_buffer[:seq_count], value_buffer[:seq_count]], axis=1)]
    pallas_call x0 -> x1, Pallas kernels: none -> 4.5 us  [attention_call(): pl.pallas_call(functools.partial(attention_kernel, scaling=scaling), out_...]
    gather x2 -> x0, local copies, waits for them, and re-layouts: 4.41 us -> none  [body(): chosen = pool[slot_of[which_half]]]
    all_to_all x1, waiting for transfers between devices: 45.7 us -> 48.2 us  [body(): lax.all_to_all(send, 'seq', split_axis=0, concat_axis=0, tiled=True)]
    another operation x6 -> x4, other arithmetic: 2.44 us -> 0.05 us  [the longest x2 1.45 us: body(): return (jnp.stack(outputs), jnp.stack(query_grads), grads[0], grads[1])]
  transfers between devices with their start and end apart: 4 -> 3, of which waited for: 4 -> 3; matrix products, arithmetic and copies ran while one was open for 5% -> 1% of each run, Pallas kernels for 0% -> 0%
where the time goes in v2:
time: 165 us; the launch traced here: 164 us
  waiting for transfers between devices  101 us (61%)
  starting transfers between devices  33.1 us (20%)
  blocking collectives  12.6 us (8%)
  local copies, waits for them, and re-layouts  7.77 us (5%)
  Pallas kernels  4.5 us (3%)
  other arithmetic  4.04 us (2%)
    all_to_all x1, waiting for transfers between devices, body(): lax.all_to_all(partials, 'seq', split_axis=0, concat_axis=0, tiled=True)  48.2 us
    all_to_all x1, waiting for transfers between devices, body(): lax.all_to_all(send, 'seq', split_axis=0, concat_axis=0, tiled=True)  48.2 us
    all_to_all x1, blocking collectives, body(): lax.all_to_all(totals, 'head', split_axis=2, concat_axis=3, tiled=True)  12.6 us
    all_to_all x1, starting transfers between devices, body(): lax.all_to_all(send, 'seq', split_axis=0, concat_axis=0, tiled=True)  12.1 us
    all_to_all x1, starting transfers between devices, body(): lax.all_to_all(partials, 'seq', split_axis=0, concat_axis=0, tiled=True)  10.9 us
    all_to_all x1, starting transfers between devices, body(): lax.all_to_all(stacked, 'head', split_axis=3, concat_axis=2, tiled=True)  10.1 us
    all_to_all x1, waiting for transfers between devices, body(): lax.all_to_all(stacked, 'head', split_axis=3, concat_axis=2, tiled=True)  4.86 us
    pallas_call x1, Pallas kernels, attention_call(): pl.pallas_call(functools.partial(attention_kernel, scaling=scaling), out_...  4.5 us
  transfers between devices with their start and end apart: 3, of which 3 were waited for; matrix products, arithmetic and copies ran while one was open for 1% of the time, Pallas kernels for 0%

profile of v2, /device:TPU:1, one launch (start us, length us, event | category | flops | bytes accessed | tf_op | source)
XLA Modules:
  0.0 164.1 jit_solution(10626157579818023983)
XLA Ops:
  0.6 0.8 pad_maximum_fusion
  1.4 0.7 copy.55
  2.1 1.7 %reshape.207 = bf16[8,2,2048]{2,1,0:T(2,128)(2,1)} reshape(bf16[1024,2,2,8]{3,2,1,0:T(2,128)(2,1)S(1)} %bitcast.49) | data formatting | bytes 131072
  3.8 10.1 %all-to-all-start = ((bf16[8,2,2048]{2,1,0:T(2,128)(2,1)}), bf16[8,2,2048]{2,1,0:T(2,128)(2,1)S(1)}, u32[]{:S(2)}, u32[]{:S(2)}) async-start(bf16[8,2,2048]{2,1,0:T(2,128)(2,1)} %reshape.207), calls=%async_computation | async-start | bytes 131072 | tf_op jit(solution)/shard_map/all_to_all | solution.py:115
  13.9 4.9 %all-to-all-done = bf16[8,2,2048]{2,1,0:T(2,128)(2,1)S(1)} async-done(((bf16[8,2,2048]{2,1,0:T(2,128)(2,1)}), bf16[8,2,2048]{2,1,0:T(2,128)(2,1)S(1)}, u32[]{:S(2)}, u32[]{:S(2)}) %all-to-all-start) | async-done | bytes 65568 | tf_op jit(solution)/shard_map/all_to_all | solution.py:115
  18.8 1.2 reshape.208
  20.0 1.3 copy.56
  21.3 1.6 broadcast_select_fusion
  22.9 12.1 %all-to-all-start.1 = ((bf16[64,2,64,128]{3,2,1,0:T(8,128)(2,1)}), bf16[64,2,64,128]{3,2,1,0:T(8,128)(2,1)S(1)}, u32[]{:S(2)}, u32[]{:S(2)}) async-start(bf16[64,2,64,128]{3,2,1,0:T(8,128)(2,1)} %broadcast_select_fusion), calls=%async_computation.1 | async-start | bytes 4194304 | tf_op jit(solution)/shard_map/all_to_all | solution.py:131
  35.0 0.1 pad_add_fusion.1
  35.1 0.0 copy-done.4
  35.1 0.2 select_reduce_fusion.1
  35.3 0.1 iota_compare_fusion.1
  35.4 0.1 iota_compare_fusion.2
  35.4 0.1 broadcast_and_fusion
  35.5 0.0 copy-done.3
  35.5 0.2 select_reduce_fusion
  35.7 0.2 fusion.6
  36.0 0.1 eq.108
  36.1 48.2 %all-to-all-done.1.recv_ref = bf16[64,2,64,128]{3,2,1,0:T(8,128)(2,1)S(1)} async-done(((bf16[64,2,64,128]{3,2,1,0:T(8,128)(2,1)}), bf16[64,2,64,128]{3,2,1,0:T(8,128)(2,1)S(1)}, u32[]{:S(2)}, u32[]{:S(2)}) %all-to-all-start.1) | async-done | bytes 2097184 | tf_op jit(solution)/shard_map/all_to_all | solution.py:131
  84.2 0.0 copy-done.1
  84.2 0.0 copy-done.2
  84.2 4.5 %shard_map.93 = (bf16[2,64,1024]{2,1,0:T(8,128)(2,1)}, bf16[2,64,1024]{2,1,0:T(8,128)(2,1)}, bf16[64,2,64,128]{3,2,1,0:T(8,128)(2,1)S(1)}, f32[2,2,64,128]{3,2,1,0:T(8,128)S(1)}) custom-call(s32[2,3,8]{2,1,0:T(4,128)S(1)} %pad_add_fusion.meta_ref, bf16[2,64,1024]{2,1,0:T(8,128)(2,1)S(1)} %copy-done.1, bf16[2,64,1024]{2,1,0:T(8,128)(2,1)S(1)} %copy-done.2, ...), custom_call_target="tpu_custom_call" | custom-call | tf_op jit(solution)/shard_map/pallas_call | solution.py:93
  88.7 1.3 copy-done
  90.1 10.9 %all-to-all-start.2 = ((bf16[64,2,64,128]{3,2,1,0:T(8,128)(2,1)}), bf16[64,2,64,128]{3,2,1,0:T(8,128)(2,1)S(1)}, u32[]{:S(2)}, u32[]{:S(2)}) async-start(bf16[64,2,64,128]{3,2,1,0:T(8,128)(2,1)} %copy-done), calls=%async_computation.2 | async-start | bytes 4194304 | tf_op jit(solution)/shard_map/all_to_all | solution.py:135
  101.0 48.2 %all-to-all-done.2 = bf16[64,2,64,128]{3,2,1,0:T(8,128)(2,1)S(1)} async-done(((bf16[64,2,64,128]{3,2,1,0:T(8,128)(2,1)}), bf16[64,2,64,128]{3,2,1,0:T(8,128)(2,1)S(1)}, u32[]{:S(2)}, u32[]{:S(2)}) %all-to-all-start.2) | async-done | bytes 2097184 | tf_op jit(solution)/shard_map/all_to_all | solution.py:135
  149.2 0.8 fusion
  150.0 0.1 copy.57
  150.1 12.6 %all_to_all.43 = bf16[2,2,64,128]{3,0,1,2:T(2,128)(2,1)S(1)} all-to-all(bf16[2,2,64,128]{3,0,1,2:T(2,128)(2,1)S(1)} %copy.57), channel_id=1, replica_groups=mesh['seq'=64,'head'=8] {'head'}, dimensions={2} | all-to-all | bytes 131072 | tf_op jit(solution)/shard_map/all_to_all | solution.py:144
  162.7 0.1 fusion.9
  162.8 0.6 copy.62
  163.4 0.6 copy.63
  (17 shorter events, 0.1 us)
Async XLA Ops:
  3.8 15.0 %all-to-all-start = ((bf16[8,2,2048]{2,1,0:T(2,128)(2,1)}), bf16[8,2,2048]{2,1,0:T(2,128)(2,1)S(1)}, u32[]{:S(2)}, u32[]{:S(2)}) async-start(bf16[8,2,2048]{2,1,0:T(2,128)(2,1)} %reshape.207), calls=%async_computation | async-start | bytes 131072 | tf_op jit(solution)/shard_map/all_to_all | solution.py:115
  22.9 12.2 %copy-start.4 = (s32[128]{0:T(128)S(1)}, s32[128]{0:T(128)}, u32[]{:S(2)}) copy-start(s32[128]{0:T(128)} %param.11) | copy-start | bytes 1540
  22.9 12.6 %copy-start.3 = (s32[4,128,8]{1,2,0:T(8,128)S(1)}, s32[4,128,8]{1,2,0:T(8,128)}, u32[]{:S(2)}) copy-start(s32[4,128,8]{1,2,0:T(8,128)} %param.10) | copy-start | bytes 49156
  22.9 61.3 %copy-start.1 = (bf16[2,64,1024]{2,1,0:T(8,128)(2,1)S(1)}, bf16[2,64,1024]{2,1,0:T(8,128)(2,1)}, u32[]{:S(2)}) copy-start(bf16[2,64,1024]{2,1,0:T(8,128)(2,1)} %q_ref.1) | copy-start | bytes 786436
  22.9 61.3 %copy-start.2 = (bf16[2,64,1024]{2,1,0:T(8,128)(2,1)S(1)}, bf16[2,64,1024]{2,1,0:T(8,128)(2,1)}, u32[]{:S(2)}) copy-start(bf16[2,64,1024]{2,1,0:T(8,128)(2,1)} %do_ref.1) | copy-start | bytes 786436
  22.9 61.3 %all-to-all-start.1 = ((bf16[64,2,64,128]{3,2,1,0:T(8,128)(2,1)}), bf16[64,2,64,128]{3,2,1,0:T(8,128)(2,1)S(1)}, u32[]{:S(2)}, u32[]{:S(2)}) async-start(bf16[64,2,64,128]{3,2,1,0:T(8,128)(2,1)} %broadcast_select_fusion), calls=%async_computation.1 | async-start | bytes 4194304 | tf_op jit(solution)/shard_map/all_to_all | solution.py:131
  88.7 1.3 copy-start
  90.1 59.1 %all-to-all-start.2 = ((bf16[64,2,64,128]{3,2,1,0:T(8,128)(2,1)}), bf16[64,2,64,128]{3,2,1,0:T(8,128)(2,1)S(1)}, u32[]{:S(2)}, u32[]{:S(2)}) async-start(bf16[64,2,64,128]{3,2,1,0:T(8,128)(2,1)} %copy-done), calls=%async_computation.2 | async-start | bytes 4194304 | tf_op jit(solution)/shard_map/all_to_all | solution.py:135

commit v3 on v2

--- a/solution.py
+++ b/solution.py
@@ -111,8 +111,13 @@
     device = lax.axis_index("seq")
     count_of_blocks = layouts.shape[1]
     halfway = count_of_blocks // 2
-    stacked = jnp.stack([key_states, value_state_rows])
-    mine = lax.all_to_all(stacked, "head", split_axis=3, concat_axis=2, tiled=True)
+    head_count = lax.axis_size("head")
+    rows = key_states.shape[1]
+    width = key_states.shape[2] // head_count
+    stacked = jnp.stack([key_states, value_state_rows]).reshape(2, 2, rows, head_count, width)
+    outgoing = jnp.transpose(stacked, (3, 0, 1, 2, 4))
+    incoming = lax.all_to_all(outgoing, "head", split_axis=0, concat_axis=0, tiled=True)
+    mine = jnp.transpose(incoming, (1, 2, 0, 3, 4)).reshape(2, 2, head_count * rows, width)
     qblocks = jnp.stack([device, count_of_blocks - 1 - device])
     pick_block = jnp.arange(count_of_blocks, dtype=jnp.int32)[None, :] == qblocks[:, None]
     plant_of = jnp.sum(jnp.where(pick_block, plant_ids[None, :], 0), axis=1)
@@ -141,7 +146,9 @@
     lower_total = own[0] + jnp.sum(back * from_higher, axis=0)
     upper_total = own[1] + jnp.sum(back * from_lower, axis=0)
     totals = jnp.stack([lower_total, upper_total], axis=1).astype(jnp.bfloat16)
-    grads = lax.all_to_all(totals, "head", split_axis=2, concat_axis=3, tiled=True)
+    outgoing = jnp.transpose(totals.reshape(2, 2, head_count, rows, width), (2, 0, 1, 3, 4))
+    incoming = lax.all_to_all(outgoing, "head", split_axis=0, concat_axis=0, tiled=True)
+    grads = jnp.transpose(incoming, (1, 2, 3, 0, 4)).reshape(2, 2, rows, head_count * width)
     return (outputs, query_grads, grads[0], grads[1])
 
 

time: 165 us -> 160 us (0.970)
  local copies, waits for them, and re-layouts: 7.77 us -> 4.18 us
    unnamed x12 -> x10, local copies, waits for them, and re-layouts: 4.26 us -> 1.35 us
where the time goes in v3:
time: 160 us
  waiting for transfers between devices  101 us (63%)
  starting transfers between devices  33.1 us (21%)
  blocking collectives  12.6 us (8%)
  Pallas kernels  4.5 us (3%)
  local copies, waits for them, and re-layouts  4.18 us (3%)
  other arithmetic  3.26 us (2%)
    all_to_all x1, waiting for transfers between devices, body(): lax.all_to_all(send, 'seq', split_axis=0, concat_axis=0, tiled=True)  48.2 us
    all_to_all x1, waiting for transfers between devices, body(): lax.all_to_all(partials, 'seq', split_axis=0, concat_axis=0, tiled=True)  48.2 us
    all_to_all x1, blocking collectives, body(): lax.all_to_all(outgoing, 'head', split_axis=0, concat_axis=0, tiled=True)  12.6 us
    all_to_all x1, starting transfers between devices, body(): lax.all_to_all(send, 'seq', split_axis=0, concat_axis=0, tiled=True)  12.1 us
    all_to_all x1, starting transfers between devices, body(): lax.all_to_all(partials, 'seq', split_axis=0, concat_axis=0, tiled=True)  10.9 us
    all_to_all x1, starting transfers between devices, body(): lax.all_to_all(outgoing, 'head', split_axis=0, concat_axis=0, tiled=True)  10.1 us
    all_to_all x1, waiting for transfers between devices, body(): lax.all_to_all(outgoing, 'head', split_axis=0, concat_axis=0, tiled=True)  4.86 us
    pallas_call x1, Pallas kernels, attention_call(): pl.pallas_call(functools.partial(attention_kernel, scaling=scaling), out_...  4.5 us
  transfers between devices with their start and end apart: 3, of which 3 were waited for; matrix products, arithmetic and copies ran while one was open for 1% of the time, Pallas kernels for 0%

profile of v3, /device:TPU:1, one launch (start us, length us, event | category | flops | bytes accessed | tf_op | source)
XLA Modules:
  0.0 159.7 jit_solution(17995883279523099499)
XLA Ops:
  0.6 0.8 copy_bitcast_fusion.1
  1.4 0.6 copy.52
  2.1 10.1 %all-to-all-start = ((bf16[8,2,2,8,128]{4,3,2,1,0:T(8,128)(2,1)}), bf16[8,2,2,8,128]{4,3,2,1,0:T(8,128)(2,1)S(1)}, u32[]{:S(2)}, u32[]{:S(2)}) async-start(bf16[8,2,2,8,128]{4,3,2,1,0:T(8,128)(2,1)} %copy.52), calls=%async_computation | async-start | bytes 131072 | tf_op jit(solution)/shard_map/all_to_all | solution.py:119
  12.2 4.9 %all-to-all-done = bf16[8,2,2,8,128]{4,3,2,1,0:T(8,128)(2,1)S(1)} async-done(((bf16[8,2,2,8,128]{4,3,2,1,0:T(8,128)(2,1)}), bf16[8,2,2,8,128]{4,3,2,1,0:T(8,128)(2,1)S(1)}, u32[]{:S(2)}, u32[]{:S(2)}) %all-to-all-start) | async-done | bytes 65568 | tf_op jit(solution)/shard_map/all_to_all | solution.py:119
  17.1 1.5 broadcast_select_fusion
  18.6 0.0 copy-start.4
  18.6 0.0 copy-start.3
  18.6 0.0 copy-start.1
  18.6 0.0 copy-start.2
  18.6 12.1 %all-to-all-start.1 = ((bf16[64,2,64,128]{3,2,1,0:T(8,128)(2,1)}), bf16[64,2,64,128]{3,2,1,0:T(8,128)(2,1)S(1)}, u32[]{:S(2)}, u32[]{:S(2)}) async-start(bf16[64,2,64,128]{3,2,1,0:T(8,128)(2,1)} %broadcast_select_fusion), calls=%async_computation.1 | async-start | bytes 4194304 | tf_op jit(solution)/shard_map/all_to_all | solution.py:136
  30.8 0.1 pad_add_fusion.1
  30.8 0.0 copy-done.4
  30.8 0.2 select_reduce_fusion.1
  31.0 0.1 iota_compare_fusion.1
  31.1 0.1 iota_compare_fusion.2
  31.2 0.1 broadcast_and_fusion
  31.3 0.0 copy-done.3
  31.3 0.2 select_reduce_fusion
  31.4 0.2 fusion.6
  31.7 0.1 eq.108
  31.8 48.2 %all-to-all-done.1.recv_ref = bf16[64,2,64,128]{3,2,1,0:T(8,128)(2,1)S(1)} async-done(((bf16[64,2,64,128]{3,2,1,0:T(8,128)(2,1)}), bf16[64,2,64,128]{3,2,1,0:T(8,128)(2,1)S(1)}, u32[]{:S(2)}, u32[]{:S(2)}) %all-to-all-start.1) | async-done | bytes 2097184 | tf_op jit(solution)/shard_map/all_to_all | solution.py:136
  80.0 0.0 copy-done.1
  80.0 0.0 copy-done.2
  80.0 4.5 %shard_map.93 = (bf16[2,64,1024]{2,1,0:T(8,128)(2,1)}, bf16[2,64,1024]{2,1,0:T(8,128)(2,1)}, bf16[64,2,64,128]{3,2,1,0:T(8,128)(2,1)S(1)}, f32[2,2,64,128]{3,2,1,0:T(8,128)S(1)}) custom-call(s32[2,3,8]{2,1,0:T(4,128)S(1)} %pad_add_fusion.meta_ref, bf16[2,64,1024]{2,1,0:T(8,128)(2,1)S(1)} %copy-done.1, bf16[2,64,1024]{2,1,0:T(8,128)(2,1)S(1)} %copy-done.2, ...), custom_call_target="tpu_custom_call" | custom-call | tf_op jit(solution)/shard_map/pallas_call | solution.py:93
  84.5 0.0 copy-start
  84.5 1.3 copy-done
  85.8 10.9 %all-to-all-start.2 = ((bf16[64,2,64,128]{3,2,1,0:T(8,128)(2,1)}), bf16[64,2,64,128]{3,2,1,0:T(8,128)(2,1)S(1)}, u32[]{:S(2)}, u32[]{:S(2)}) async-start(bf16[64,2,64,128]{3,2,1,0:T(8,128)(2,1)} %copy-done), calls=%async_computation.2 | async-start | bytes 4194304 | tf_op jit(solution)/shard_map/all_to_all | solution.py:140
  96.7 48.2 %all-to-all-done.2 = bf16[64,2,64,128]{3,2,1,0:T(8,128)(2,1)S(1)} async-done(((bf16[64,2,64,128]{3,2,1,0:T(8,128)(2,1)}), bf16[64,2,64,128]{3,2,1,0:T(8,128)(2,1)S(1)}, u32[]{:S(2)}, u32[]{:S(2)}) %all-to-all-start.2) | async-done | bytes 2097184 | tf_op jit(solution)/shard_map/all_to_all | solution.py:140
  144.9 0.8 fusion
  145.7 12.6 %all_to_all.20 = bf16[8,2,2,8,128]{4,3,1,2,0:T(8,128)(2,1)S(1)} all-to-all(bf16[8,2,2,8,128]{4,3,1,2,0:T(8,128)(2,1)S(1)} %copy.54), channel_id=1, replica_groups=mesh['seq'=64,'head'=8] {'head'}, dimensions={0} | all-to-all | bytes 131072 | tf_op jit(solution)/shard_map/all_to_all | solution.py:150
  158.4 0.6 squeeze.14
  159.0 0.6 squeeze.15
  (18 shorter events, 0.2 us)
Async XLA Ops:
  2.1 15.0 %all-to-all-start = ((bf16[8,2,2,8,128]{4,3,2,1,0:T(8,128)(2,1)}), bf16[8,2,2,8,128]{4,3,2,1,0:T(8,128)(2,1)S(1)}, u32[]{:S(2)}, u32[]{:S(2)}) async-start(bf16[8,2,2,8,128]{4,3,2,1,0:T(8,128)(2,1)} %copy.52), calls=%async_computation | async-start | bytes 131072 | tf_op jit(solution)/shard_map/all_to_all | solution.py:119
  18.6 12.2 %copy-start.4 = (s32[128]{0:T(128)S(1)}, s32[128]{0:T(128)}, u32[]{:S(2)}) copy-start(s32[128]{0:T(128)} %param.11) | copy-start | bytes 1540
  18.6 12.6 %copy-start.3 = (s32[4,128,8]{1,2,0:T(8,128)S(1)}, s32[4,128,8]{1,2,0:T(8,128)}, u32[]{:S(2)}) copy-start(s32[4,128,8]{1,2,0:T(8,128)} %param.10) | copy-start | bytes 49156
  18.6 61.3 %copy-start.1 = (bf16[2,64,1024]{2,1,0:T(8,128)(2,1)S(1)}, bf16[2,64,1024]{2,1,0:T(8,128)(2,1)}, u32[]{:S(2)}) copy-start(bf16[2,64,1024]{2,1,0:T(8,128)(2,1)} %q_ref.1) | copy-start | bytes 786436
  18.6 61.3 %copy-start.2 = (bf16[2,64,1024]{2,1,0:T(8,128)(2,1)S(1)}, bf16[2,64,1024]{2,1,0:T(8,128)(2,1)}, u32[]{:S(2)}) copy-start(bf16[2,64,1024]{2,1,0:T(8,128)(2,1)} %do_ref.1) | copy-start | bytes 786436
  18.6 61.3 %all-to-all-start.1 = ((bf16[64,2,64,128]{3,2,1,0:T(8,128)(2,1)}), bf16[64,2,64,128]{3,2,1,0:T(8,128)(2,1)S(1)}, u32[]{:S(2)}, u32[]{:S(2)}) async-start(bf16[64,2,64,128]{3,2,1,0:T(8,128)(2,1)} %broadcast_select_fusion), calls=%async_computation.1 | async-start | bytes 4194304 | tf_op jit(solution)/shard_map/all_to_all | solution.py:136
  84.5 1.3 copy-start
  85.8 59.1 %all-to-all-start.2 = ((bf16[64,2,64,128]{3,2,1,0:T(8,128)(2,1)}), bf16[64,2,64,128]{3,2,1,0:T(8,128)(2,1)S(1)}, u32[]{:S(2)}, u32[]{:S(2)}) async-start(bf16[64,2,64,128]{3,2,1,0:T(8,128)(2,1)} %copy-done), calls=%async_computation.2 | async-start | bytes 4194304 | tf_op jit(solution)/shard_map/all_to_all | solution.py:140

commit v4 on v3

--- a/solution.py
+++ b/solution.py
@@ -27,12 +27,17 @@
 
 
 def attention_kernel(meta_ref, q_ref, do_ref, recv_ref, mine_ref,
-                     out_ref, dq_ref, send_ref, own_ref, acc_ref, *, scaling):
+                     out_ref, dq_ref, send_hbm, own_ref, acc_ref, send_ref, sem, *, scaling):
     seq_count = recv_ref.shape[0]
     groups = q_ref.shape[2] // HEAD_SIZE
     rows = groups * BLOCK_TOKENS_N
     cols = KEY_LIST_SIZE * BLOCK_TOKENS_N
-    acc_ref[...] = jnp.zeros_like(acc_ref)
+    for half in range(2):
+        for j in range(KEY_LIST_SIZE):
+            acc_ref[meta_ref[half, 0, j]] = jnp.zeros(acc_ref.shape[1:], acc_ref.dtype)
+    acc_ref[seq_count] = jnp.zeros(acc_ref.shape[1:], acc_ref.dtype)
+    acc_ref[seq_count + 1] = jnp.zeros(acc_ref.shape[1:], acc_ref.dtype)
+    send_ref[...] = jnp.zeros_like(send_ref)
     col = lax.broadcasted_iota(jnp.int32, (1, cols), 1)
     col_block = col // BLOCK_TOKENS_N
     key_pos = col % BLOCK_TOKENS_N
@@ -81,8 +86,19 @@
             piece = slice(j * BLOCK_TOKENS_N, (j + 1) * BLOCK_TOKENS_N)
             acc_ref[slot, 0] += jnp.where(keep, key_portion[piece], 0.0)
             acc_ref[slot, 1] += jnp.where(keep, value_portion[piece], 0.0)
-    send_ref[...] = acc_ref[:seq_count].astype(send_ref.dtype)
+    for half in range(2):
+        for j in range(KEY_LIST_SIZE):
+            slot = meta_ref[half, 0, j]
+            r = jnp.minimum(slot, seq_count - 1)
+
+            @pl.when(slot < seq_count)
+            def _():
+                send_ref[r] = acc_ref[r].astype(send_ref.dtype)
+
+    copy = pltpu.make_async_copy(send_ref, send_hbm, sem)
+    copy.start()
     own_ref[...] = acc_ref[seq_count:]
+    copy.wait()
 
 
 def attention_call(meta, queries, grad_out, received, mine, scaling):
@@ -99,8 +115,17 @@
             jax.ShapeDtypeStruct((2, 2, BLOCK_TOKENS_N, width), jnp.float32),
         ),
         in_specs=[pl.BlockSpec(memory_space=smem)] + [pl.BlockSpec(memory_space=vmem)] * 4,
-        out_specs=[pl.BlockSpec(memory_space=vmem)] * 4,
-        scratch_shapes=[pltpu.VMEM((seq_count + 2, 2, BLOCK_TOKENS_N, width), jnp.float32)],
+        out_specs=[
+            pl.BlockSpec(memory_space=vmem),
+            pl.BlockSpec(memory_space=vmem),
+            pl.BlockSpec(memory_space=pl.ANY),
+            pl.BlockSpec(memory_space=vmem),
+        ],
+        scratch_shapes=[
+            pltpu.VMEM((seq_count + 2, 2, BLOCK_TOKENS_N, width), jnp.float32),
+            pltpu.VMEM(received.shape, received.dtype),
+            pltpu.SemaphoreType.DMA(()),
+        ],
         compiler_params=pltpu.CompilerParams(vmem_limit_bytes=48 * 1024 * 1024),
     )(meta, queries, grad_out, received, mine)
 

time: 160 us -> 161 us (level)
  no operation moved by 1% of the time
where the time goes in v4:
time: 161 us; the launch traced here: 160 us
  waiting for transfers between devices  101 us (63%)
  starting transfers between devices  33.1 us (21%)
  blocking collectives  12.7 us (8%)
  Pallas kernels  4.92 us (3%)
  local copies, waits for them, and re-layouts  4.18 us (3%)
  other arithmetic  3.26 us (2%)
    all_to_all x1, waiting for transfers between devices, body(): lax.all_to_all(send, 'seq', split_axis=0, concat_axis=0, tiled=True)  48.2 us
    all_to_all x1, waiting for transfers between devices, body(): lax.all_to_all(partials, 'seq', split_axis=0, concat_axis=0, tiled=True)  48.1 us
    all_to_all x1, blocking collectives, body(): lax.all_to_all(outgoing, 'head', split_axis=0, concat_axis=0, tiled=True)  12.7 us
    all_to_all x1, starting transfers between devices, body(): lax.all_to_all(send, 'seq', split_axis=0, concat_axis=0, tiled=True)  12.1 us
    all_to_all x1, starting transfers between devices, body(): lax.all_to_all(partials, 'seq', split_axis=0, concat_axis=0, tiled=True)  10.9 us
    all_to_all x1, starting transfers between devices, body(): lax.all_to_all(outgoing, 'head', split_axis=0, concat_axis=0, tiled=True)  10.1 us
    pallas_call x1, Pallas kernels, attention_call(): pl.pallas_call(functools.partial(attention_kernel, scaling=scaling), out_...  4.92 us
    all_to_all x1, waiting for transfers between devices, body(): lax.all_to_all(outgoing, 'head', split_axis=0, concat_axis=0, tiled=True)  4.86 us
  transfers between devices with their start and end apart: 3, of which 3 were waited for; matrix products, arithmetic and copies ran while one was open for 1% of the time, Pallas kernels for 0%

profile of v4, /device:TPU:1, one launch (start us, length us, event | category | flops | bytes accessed | tf_op | source)
XLA Modules:
  0.0 160.1 jit_solution(5909714232614825610)
XLA Ops:
  0.6 0.8 copy_bitcast_fusion.1
  1.4 0.6 copy.52
  2.1 10.1 %all-to-all-start = ((bf16[8,2,2,8,128]{4,3,2,1,0:T(8,128)(2,1)}), bf16[8,2,2,8,128]{4,3,2,1,0:T(8,128)(2,1)S(1)}, u32[]{:S(2)}, u32[]{:S(2)}) async-start(bf16[8,2,2,8,128]{4,3,2,1,0:T(8,128)(2,1)} %copy.52), calls=%async_computation | async-start | bytes 131072 | tf_op jit(solution)/shard_map/all_to_all | solution.py:144
  12.2 4.9 %all-to-all-done = bf16[8,2,2,8,128]{4,3,2,1,0:T(8,128)(2,1)S(1)} async-done(((bf16[8,2,2,8,128]{4,3,2,1,0:T(8,128)(2,1)}), bf16[8,2,2,8,128]{4,3,2,1,0:T(8,128)(2,1)S(1)}, u32[]{:S(2)}, u32[]{:S(2)}) %all-to-all-start) | async-done | bytes 65568 | tf_op jit(solution)/shard_map/all_to_all | solution.py:144
  17.1 1.5 broadcast_select_fusion
  18.6 0.0 copy-start.4
  18.6 0.0 copy-start.3
  18.6 0.0 copy-start.1
  18.6 0.0 copy-start.2
  18.6 12.1 %all-to-all-start.1 = ((bf16[64,2,64,128]{3,2,1,0:T(8,128)(2,1)}), bf16[64,2,64,128]{3,2,1,0:T(8,128)(2,1)S(1)}, u32[]{:S(2)}, u32[]{:S(2)}) async-start(bf16[64,2,64,128]{3,2,1,0:T(8,128)(2,1)} %broadcast_select_fusion), calls=%async_computation.1 | async-start | bytes 4194304 | tf_op jit(solution)/shard_map/all_to_all | solution.py:161
  30.8 0.1 pad_add_fusion.1
  30.8 0.0 copy-done.4
  30.8 0.2 select_reduce_fusion.1
  31.0 0.1 iota_compare_fusion.1
  31.1 0.1 iota_compare_fusion.2
  31.2 0.1 broadcast_and_fusion
  31.3 0.0 copy-done.3
  31.3 0.2 select_reduce_fusion
  31.4 0.2 fusion.6
  31.7 0.1 eq.108
  31.8 48.2 %all-to-all-done.1.recv_ref = bf16[64,2,64,128]{3,2,1,0:T(8,128)(2,1)S(1)} async-done(((bf16[64,2,64,128]{3,2,1,0:T(8,128)(2,1)}), bf16[64,2,64,128]{3,2,1,0:T(8,128)(2,1)S(1)}, u32[]{:S(2)}, u32[]{:S(2)}) %all-to-all-start.1) | async-done | bytes 2097184 | tf_op jit(solution)/shard_map/all_to_all | solution.py:161
  80.0 0.0 copy-done.1
  80.0 0.0 copy-done.2
  80.0 4.9 %shard_map.93 = (bf16[2,64,1024]{2,1,0:T(8,128)(2,1)}, bf16[2,64,1024]{2,1,0:T(8,128)(2,1)}, bf16[64,2,64,128]{3,2,1,0:T(8,128)(2,1)S(1)}, f32[2,2,64,128]{3,2,1,0:T(8,128)S(1)}) custom-call(s32[2,3,8]{2,1,0:T(4,128)S(1)} %pad_add_fusion.meta_ref, bf16[2,64,1024]{2,1,0:T(8,128)(2,1)S(1)} %copy-done.1, bf16[2,64,1024]{2,1,0:T(8,128)(2,1)S(1)} %copy-done.2, ...), custom_call_target="tpu_custom_call" | custom-call | tf_op jit(solution)/shard_map/pallas_call | solution.py:109
  84.9 0.0 copy-start
  84.9 1.3 copy-done
  86.2 10.9 %all-to-all-start.2 = ((bf16[64,2,64,128]{3,2,1,0:T(8,128)(2,1)}), bf16[64,2,64,128]{3,2,1,0:T(8,128)(2,1)S(1)}, u32[]{:S(2)}, u32[]{:S(2)}) async-start(bf16[64,2,64,128]{3,2,1,0:T(8,128)(2,1)} %copy-done), calls=%async_computation.2 | async-start | bytes 4194304 | tf_op jit(solution)/shard_map/all_to_all | solution.py:165
  97.2 48.1 %all-to-all-done.2 = bf16[64,2,64,128]{3,2,1,0:T(8,128)(2,1)S(1)} async-done(((bf16[64,2,64,128]{3,2,1,0:T(8,128)(2,1)}), bf16[64,2,64,128]{3,2,1,0:T(8,128)(2,1)S(1)}, u32[]{:S(2)}, u32[]{:S(2)}) %all-to-all-start.2) | async-done | bytes 2097184 | tf_op jit(solution)/shard_map/all_to_all | solution.py:165
  145.3 0.8 fusion
  146.1 12.7 %all_to_all.20 = bf16[8,2,2,8,128]{4,3,1,2,0:T(8,128)(2,1)S(1)} all-to-all(bf16[8,2,2,8,128]{4,3,1,2,0:T(8,128)(2,1)S(1)} %copy.54), channel_id=1, replica_groups=mesh['seq'=64,'head'=8] {'head'}, dimensions={0} | all-to-all | bytes 131072 | tf_op jit(solution)/shard_map/all_to_all | solution.py:175
  158.8 0.6 squeeze.14
  159.5 0.6 squeeze.15
  (18 shorter events, 0.2 us)
Async XLA Ops:
  2.1 15.0 %all-to-all-start = ((bf16[8,2,2,8,128]{4,3,2,1,0:T(8,128)(2,1)}), bf16[8,2,2,8,128]{4,3,2,1,0:T(8,128)(2,1)S(1)}, u32[]{:S(2)}, u32[]{:S(2)}) async-start(bf16[8,2,2,8,128]{4,3,2,1,0:T(8,128)(2,1)} %copy.52), calls=%async_computation | async-start | bytes 131072 | tf_op jit(solution)/shard_map/all_to_all | solution.py:144
  18.6 12.2 %copy-start.4 = (s32[128]{0:T(128)S(1)}, s32[128]{0:T(128)}, u32[]{:S(2)}) copy-start(s32[128]{0:T(128)} %param.11) | copy-start | bytes 1540
  18.6 12.6 %copy-start.3 = (s32[4,128,8]{1,2,0:T(8,128)S(1)}, s32[4,128,8]{1,2,0:T(8,128)}, u32[]{:S(2)}) copy-start(s32[4,128,8]{1,2,0:T(8,128)} %param.10) | copy-start | bytes 49156
  18.6 61.3 %copy-start.1 = (bf16[2,64,1024]{2,1,0:T(8,128)(2,1)S(1)}, bf16[2,64,1024]{2,1,0:T(8,128)(2,1)}, u32[]{:S(2)}) copy-start(bf16[2,64,1024]{2,1,0:T(8,128)(2,1)} %q_ref.1) | copy-start | bytes 786436
  18.6 61.3 %copy-start.2 = (bf16[2,64,1024]{2,1,0:T(8,128)(2,1)S(1)}, bf16[2,64,1024]{2,1,0:T(8,128)(2,1)}, u32[]{:S(2)}) copy-start(bf16[2,64,1024]{2,1,0:T(8,128)(2,1)} %do_ref.1) | copy-start | bytes 786436
  18.6 61.3 %all-to-all-start.1 = ((bf16[64,2,64,128]{3,2,1,0:T(8,128)(2,1)}), bf16[64,2,64,128]{3,2,1,0:T(8,128)(2,1)S(1)}, u32[]{:S(2)}, u32[]{:S(2)}) async-start(bf16[64,2,64,128]{3,2,1,0:T(8,128)(2,1)} %broadcast_select_fusion), calls=%async_computation.1 | async-start | bytes 4194304 | tf_op jit(solution)/shard_map/all_to_all | solution.py:161
  84.9 1.3 copy-start
  86.2 59.1 %all-to-all-start.2 = ((bf16[64,2,64,128]{3,2,1,0:T(8,128)(2,1)}), bf16[64,2,64,128]{3,2,1,0:T(8,128)(2,1)S(1)}, u32[]{:S(2)}, u32[]{:S(2)}) async-start(bf16[64,2,64,128]{3,2,1,0:T(8,128)(2,1)} %copy-done), calls=%async_computation.2 | async-start | bytes 4194304 | tf_op jit(solution)/shard_map/all_to_all | solution.py:165

commit v5 on v3

--- a/solution.py
+++ b/solution.py
@@ -32,7 +32,9 @@
     groups = q_ref.shape[2] // HEAD_SIZE
     rows = groups * BLOCK_TOKENS_N
     cols = KEY_LIST_SIZE * BLOCK_TOKENS_N
-    acc_ref[...] = jnp.zeros_like(acc_ref)
+    for half in range(2):
+        for j in range(KEY_LIST_SIZE):
+            acc_ref[meta_ref[half, 0, j]] = jnp.zeros(acc_ref.shape[1:], acc_ref.dtype)
     col = lax.broadcasted_iota(jnp.int32, (1, cols), 1)
     col_block = col // BLOCK_TOKENS_N
     key_pos = col % BLOCK_TOKENS_N
@@ -81,7 +83,10 @@
             piece = slice(j * BLOCK_TOKENS_N, (j + 1) * BLOCK_TOKENS_N)
             acc_ref[slot, 0] += jnp.where(keep, key_portion[piece], 0.0)
             acc_ref[slot, 1] += jnp.where(keep, value_portion[piece], 0.0)
-    send_ref[...] = acc_ref[:seq_count].astype(send_ref.dtype)
+    for half in range(2):
+        for j in range(KEY_LIST_SIZE):
+            r = jnp.minimum(meta_ref[half, 0, j], seq_count - 1)
+            send_ref[r] = acc_ref[r].astype(send_ref.dtype)
     own_ref[...] = acc_ref[seq_count:]
 
 
@@ -141,10 +146,15 @@
         jnp.float32
     )
     source = jnp.arange(seq_count, dtype=jnp.int32)
-    from_higher = (source > device).astype(jnp.float32)[:, None, None, None]
-    from_lower = (source < device).astype(jnp.float32)[:, None, None, None]
-    lower_total = own[0] + jnp.sum(back * from_higher, axis=0)
-    upper_total = own[1] + jnp.sum(back * from_lower, axis=0)
+    sender_blocks = jnp.stack([source, count_of_blocks - 1 - source], axis=1)
+    sender_plants = plant_ids[sender_blocks]
+    sender_lists = layouts[sender_plants, sender_blocks].reshape(seq_count, -1)
+    wanted = jnp.where(source > device, device, count_of_blocks - 1 - device)
+    listed_here = jnp.any(sender_lists == wanted[:, None], axis=1) & (source != device)
+    from_higher = (listed_here & (source > device))[:, None, None, None]
+    from_lower = (listed_here & (source < device))[:, None, None, None]
+    lower_total = own[0] + jnp.sum(jnp.where(from_higher, back, 0.0), axis=0)
+    upper_total = own[1] + jnp.sum(jnp.where(from_lower, back, 0.0), axis=0)
     totals = jnp.stack([lower_total, upper_total], axis=1).astype(jnp.bfloat16)
     outgoing = jnp.transpose(totals.reshape(2, 2, head_count, rows, width), (2, 0, 1, 3, 4))
     incoming = lax.all_to_all(outgoing, "head", split_axis=0, concat_axis=0, tiled=True)

time: 160 us -> 160 us (level)
  waiting for transfers between devices: 101 us -> 96.5 us
  local copies, waits for them, and re-layouts: 4.18 us -> 7.45 us
    all_to_all x1, waiting for transfers between devices: 48.2 us -> 43.5 us  [body(): lax.all_to_all(partials, 'seq', split_axis=0, concat_axis=0, tiled=True)]
    gather x0 -> x4, local copies, waits for them, and re-layouts: none -> 2.65 us  [the longest x3 1.42 us: body(): sender_plants = plant_ids[sender_blocks]]
  transfers between devices with their start and end apart: 3 -> 3, of which waited for: 3 -> 3; matrix products, arithmetic and copies ran while one was open for 1% -> 4% of each run, Pallas kernels for 0% -> 0%
where the time goes in v5:
time: 160 us
  waiting for transfers between devices  96.5 us (60%)
  starting transfers between devices  33.1 us (21%)
  blocking collectives  12.6 us (8%)
  local copies, waits for them, and re-layouts  7.45 us (5%)
  other arithmetic  4.65 us (3%)
  Pallas kernels  4.29 us (3%)
    all_to_all x1, waiting for transfers between devices, body(): lax.all_to_all(send, 'seq', split_axis=0, concat_axis=0, tiled=True)  48.2 us
    all_to_all x1, waiting for transfers between devices, body(): lax.all_to_all(partials, 'seq', split_axis=0, concat_axis=0, tiled=True)  43.5 us
    all_to_all x1, blocking collectives, body(): lax.all_to_all(outgoing, 'head', split_axis=0, concat_axis=0, tiled=True)  12.6 us
    all_to_all x1, starting transfers between devices, body(): lax.all_to_all(send, 'seq', split_axis=0, concat_axis=0, tiled=True)  12.1 us
    all_to_all x1, starting transfers between devices, body(): lax.all_to_all(partials, 'seq', split_axis=0, concat_axis=0, tiled=True)  10.9 us
    all_to_all x1, starting transfers between devices, body(): lax.all_to_all(outgoing, 'head', split_axis=0, concat_axis=0, tiled=True)  10.1 us
    all_to_all x1, waiting for transfers between devices, body(): lax.all_to_all(outgoing, 'head', split_axis=0, concat_axis=0, tiled=True)  4.86 us
    pallas_call x1, Pallas kernels, attention_call(): pl.pallas_call(functools.partial(attention_kernel, scaling=scaling), out_...  4.29 us
  transfers between devices with their start and end apart: 3, of which 3 were waited for; matrix products, arithmetic and copies ran while one was open for 4% of the time, Pallas kernels for 0%

profile of v5, /device:TPU:1, one launch (start us, length us, event | category | flops | bytes accessed | tf_op | source)
XLA Modules:
  0.0 159.5 jit_solution(8436127190775904776)
XLA Ops:
  0.6 0.8 copy_bitcast_fusion.1
  1.4 0.6 copy.88
  2.1 10.1 %all-to-all-start = ((bf16[8,2,2,8,128]{4,3,2,1,0:T(8,128)(2,1)}), bf16[8,2,2,8,128]{4,3,2,1,0:T(8,128)(2,1)S(1)}, u32[]{:S(2)}, u32[]{:S(2)}) async-start(bf16[8,2,2,8,128]{4,3,2,1,0:T(8,128)(2,1)} %copy.88), calls=%async_computation | async-start | bytes 131072 | tf_op jit(solution)/shard_map/all_to_all | solution.py:124
  12.2 4.9 %all-to-all-done = bf16[8,2,2,8,128]{4,3,2,1,0:T(8,128)(2,1)S(1)} async-done(((bf16[8,2,2,8,128]{4,3,2,1,0:T(8,128)(2,1)}), bf16[8,2,2,8,128]{4,3,2,1,0:T(8,128)(2,1)S(1)}, u32[]{:S(2)}, u32[]{:S(2)}) %all-to-all-start) | async-done | bytes 65568 | tf_op jit(solution)/shard_map/all_to_all | solution.py:124
  17.1 1.6 broadcast_select_fusion
  18.6 12.1 %all-to-all-start.1 = ((bf16[64,2,64,128]{3,2,1,0:T(8,128)(2,1)}), bf16[64,2,64,128]{3,2,1,0:T(8,128)(2,1)S(1)}, u32[]{:S(2)}, u32[]{:S(2)}) async-start(bf16[64,2,64,128]{3,2,1,0:T(8,128)(2,1)} %broadcast_select_fusion), calls=%async_computation.1 | async-start | bytes 4194304 | tf_op jit(solution)/shard_map/all_to_all | solution.py:141
  30.8 0.1 pad_add_fusion.1
  30.9 0.2 select_reduce_fusion.1
  31.0 0.1 iota_compare_fusion.1
  31.1 0.1 iota_compare_fusion.2
  31.2 0.1 broadcast_and_fusion
  31.3 0.2 select_reduce_fusion
  31.4 0.2 fusion.6
  31.8 48.2 %all-to-all-done.1.recv_ref = bf16[64,2,64,128]{3,2,1,0:T(8,128)(2,1)S(1)} async-done(((bf16[64,2,64,128]{3,2,1,0:T(8,128)(2,1)}), bf16[64,2,64,128]{3,2,1,0:T(8,128)(2,1)S(1)}, u32[]{:S(2)}, u32[]{:S(2)}) %all-to-all-start.1) | async-done | bytes 2097184 | tf_op jit(solution)/shard_map/all_to_all | solution.py:141
  80.0 4.3 %shard_map.93 = (bf16[2,64,1024]{2,1,0:T(8,128)(2,1)}, bf16[2,64,1024]{2,1,0:T(8,128)(2,1)}, bf16[64,2,64,128]{3,2,1,0:T(8,128)(2,1)S(1)}, f32[2,2,64,128]{3,2,1,0:T(8,128)S(1)}) custom-call(s32[2,3,8]{2,1,0:T(4,128)S(1)} %pad_add_fusion.meta_ref, bf16[2,64,1024]{2,1,0:T(8,128)(2,1)S(1)} %copy-done.1, bf16[2,64,1024]{2,1,0:T(8,128)(2,1)S(1)} %copy-done.2, ...), custom_call_target="tpu_custom_call" | custom-call | tf_op jit(solution)/shard_map/pallas_call | solution.py:98
  84.3 1.3 copy-done
  85.6 10.9 %all-to-all-start.2 = ((bf16[64,2,64,128]{3,2,1,0:T(8,128)(2,1)}), bf16[64,2,64,128]{3,2,1,0:T(8,128)(2,1)S(1)}, u32[]{:S(2)}, u32[]{:S(2)}) async-start(bf16[64,2,64,128]{3,2,1,0:T(8,128)(2,1)} %copy-done), calls=%async_computation.2 | async-start | bytes 4194304 | tf_op jit(solution)/shard_map/all_to_all | solution.py:145
  96.5 0.1 copy.95
  96.7 0.1 copy.90
  96.8 0.1 reshape.319
  96.9 1.2 gather_fusion
  98.2 0.1 gather.9
  98.3 0.1 copy.91
  98.4 0.1 copy.94
  98.5 0.1 reshape.325
  98.7 1.2 gather_fusion.1
  99.9 1.3 compare_reduce_fusion
  101.2 43.5 %all-to-all-done.2 = bf16[64,2,64,128]{3,2,1,0:T(8,128)(2,1)S(1)} async-done(((bf16[64,2,64,128]{3,2,1,0:T(8,128)(2,1)}), bf16[64,2,64,128]{3,2,1,0:T(8,128)(2,1)S(1)}, u32[]{:S(2)}, u32[]{:S(2)}) %all-to-all-start.2) | async-done | bytes 2097184 | tf_op jit(solution)/shard_map/all_to_all | solution.py:145
  144.7 0.8 fusion
  145.6 12.6 %all_to_all.20 = bf16[8,2,2,8,128]{4,3,1,2,0:T(8,128)(2,1)S(1)} all-to-all(bf16[8,2,2,8,128]{4,3,1,2,0:T(8,128)(2,1)S(1)} %copy.96), channel_id=1, replica_groups=mesh['seq'=64,'head'=8] {'head'}, dimensions={0} | all-to-all | bytes 131072 | tf_op jit(solution)/shard_map/all_to_all | solution.py:160
  158.2 0.6 squeeze.15
  158.9 0.6 squeeze.14
  (34 shorter events, 0.3 us)
Async XLA Ops:
  2.1 15.0 %all-to-all-start = ((bf16[8,2,2,8,128]{4,3,2,1,0:T(8,128)(2,1)}), bf16[8,2,2,8,128]{4,3,2,1,0:T(8,128)(2,1)S(1)}, u32[]{:S(2)}, u32[]{:S(2)}) async-start(bf16[8,2,2,8,128]{4,3,2,1,0:T(8,128)(2,1)} %copy.88), calls=%async_computation | async-start | bytes 131072 | tf_op jit(solution)/shard_map/all_to_all | solution.py:124
  18.6 12.2 %copy-start.3 = (s32[128]{0:T(128)S(1)}, s32[128]{0:T(128)}, u32[]{:S(2)}) copy-start(s32[128]{0:T(128)} %param.11) | copy-start | bytes 1540
  18.6 12.6 %copy-start.4 = (s32[4,128,8]{1,2,0:T(8,128)S(1)}, s32[4,128,8]{1,2,0:T(8,128)}, u32[]{:S(2)}) copy-start(s32[4,128,8]{1,2,0:T(8,128)} %param.10) | copy-start | bytes 49156
  18.6 61.3 %copy-start.1 = (bf16[2,64,1024]{2,1,0:T(8,128)(2,1)S(1)}, bf16[2,64,1024]{2,1,0:T(8,128)(2,1)}, u32[]{:S(2)}) copy-start(bf16[2,64,1024]{2,1,0:T(8,128)(2,1)} %q_ref.1) | copy-start | bytes 786436
  18.6 61.3 %copy-start.2 = (bf16[2,64,1024]{2,1,0:T(8,128)(2,1)S(1)}, bf16[2,64,1024]{2,1,0:T(8,128)(2,1)}, u32[]{:S(2)}) copy-start(bf16[2,64,1024]{2,1,0:T(8,128)(2,1)} %do_ref.1) | copy-start | bytes 786436
  18.6 61.3 %all-to-all-start.1 = ((bf16[64,2,64,128]{3,2,1,0:T(8,128)(2,1)}), bf16[64,2,64,128]{3,2,1,0:T(8,128)(2,1)S(1)}, u32[]{:S(2)}, u32[]{:S(2)}) async-start(bf16[64,2,64,128]{3,2,1,0:T(8,128)(2,1)} %broadcast_select_fusion), calls=%async_computation.1 | async-start | bytes 4194304 | tf_op jit(solution)/shard_map/all_to_all | solution.py:141
  84.3 1.4 copy-start
  85.6 59.1 %all-to-all-start.2 = ((bf16[64,2,64,128]{3,2,1,0:T(8,128)(2,1)}), bf16[64,2,64,128]{3,2,1,0:T(8,128)(2,1)S(1)}, u32[]{:S(2)}, u32[]{:S(2)}) async-start(bf16[64,2,64,128]{3,2,1,0:T(8,128)(2,1)} %copy-done), calls=%async_computation.2 | async-start | bytes 4194304 | tf_op jit(solution)/shard_map/all_to_all | solution.py:145
